TPU v7x, 256 devices: a whole 4x4x8 slice. The times are simulated.
256 devices in a mesh: eg: 16 (over x_hi, z), blk: 16 (over x_lo, y, core).
Axes of the slice: x: 4 (x_hi: 2, x_lo: 2; x = x_hi * 2 + x_lo), y: 4, z: 8, core: 2. Of those that a mesh axis runs over, the one named last changes fastest.
Arguments:
- tokens: bfloat16 [2048, 7168], P(('eg', 'blk')), may hold values from -6 to 6
- grad_out: bfloat16 [2048, 7168], P(('eg', 'blk')), may hold values from -4 to 4
- expert_ids: int32 [2048, 2], P(('eg', 'blk')), may hold values from 0 to 15, all different within a row; in each aligned block of 8 rows (0 to 7, 8 to 15, ...) at most 2 rows name the same one
- gate_weights: bfloat16 [2048, 2], P(('eg', 'blk')), may hold values from 0.049804688 to 1
- gate_codes: bfloat16 [16, 7168, 2048], P('eg', None, 'blk'), may hold values from -0.0625 to 0.0625
- up_codes: bfloat16 [16, 7168, 2048], P('eg', None, 'blk'), may hold values from -0.0625 to 0.0625
- down_codes: bfloat16 [16, 7168, 2048], P('eg', None, 'blk'), may hold values from -0.125 to 0.125
- block_scales: bfloat16 [16, 3, 16, 56], P('eg', None, 'blk'), may hold values from 0.29882812 to 3
Outputs:
- grad_tokens: bfloat16 [2048, 7168], P(('eg', 'blk'))
- grad_gates: bfloat16 [2048, 2], P(('eg', 'blk'))
- gate_grad: bfloat16 [16, 7168, 2048], P('eg', None, 'blk')
- up_grad: bfloat16 [16, 7168, 2048], P('eg', None, 'blk')
- down_grad: bfloat16 [16, 7168, 2048], P('eg', None, 'blk')
Inputs may be any that keep to these rules, and one draw needn't show every extreme that they name: `expert_ids`: each token names 2 different experts. Among the 8 tokens of one device (aligned blocks of rows) at most 2 name the same expert, and in every draw some device's tokens reach 2 for some expert.
All inputs are finite; a program needn't handle non-finite values.
Results may differ from a plain program's by a relative error of at most 0.028.
Values may be sent and summed in bfloat16 or wider, within the bound.
No kernel may reach another device: no remote copies, remote signals or barrier semaphores. Data moves between devices by JAX's collectives and lax.ppermute only.
A program may use at most 128 MiB of HBM per device.

v0:
```python
import jax
import jax.numpy as jnp
from jax import lax
from jax.sharding import PartitionSpec as P

QBLOCK = 128
TOPK = 2


def dequantize(codes, scales):
    rows_in, cols_in = codes.shape
    blocks = codes.astype(jnp.float32).reshape(rows_in // QBLOCK, QBLOCK, cols_in // QBLOCK, QBLOCK)
    scaled = blocks * jnp.transpose(scales.astype(jnp.float32))[:, None, :, None]
    return scaled.reshape(rows_in, cols_in).astype(jnp.bfloat16)


def backward_math(gate_pre, up_pre, down_back, gates):
    sigma = jax.nn.sigmoid(gate_pre)
    hidden = gate_pre * sigma * up_pre
    grad_hidden = gates[:, None] * down_back
    grad_up = (grad_hidden * gate_pre * sigma).astype(jnp.bfloat16)
    grad_gate = (grad_hidden * up_pre * sigma * (1.0 + gate_pre * (1.0 - sigma))).astype(
        jnp.bfloat16
    )
    gated_hidden = (gates[:, None] * hidden).astype(jnp.bfloat16)
    return (hidden, grad_gate, grad_up, gated_hidden)


def routing_tables(expert_ids, experts, capacity):
    route_hot = (
        expert_ids[:, :, None] == jnp.arange(experts, dtype=jnp.int32)[None, None, :]
    ).astype(jnp.int32)
    chosen = jnp.sum(route_hot, axis=1)
    earlier = jnp.cumsum(chosen, axis=0) - chosen
    slot_hot = (earlier[:, :, None] == jnp.arange(capacity, dtype=jnp.int32)[None, None, :]).astype(
        jnp.int32
    )
    placed = chosen[:, :, None] * slot_hot
    picked = route_hot[:, :, :, None] * slot_hot[:, None, :, :]
    return (placed.astype(jnp.float32), picked.astype(jnp.float32))


def project_back(grad_gate, grad_up, wgate, wup):
    contract_cols = (((1,), (1,)), ((), ()))
    partial_value = lax.dot_general(
        grad_gate, wgate, contract_cols, preferred_element_type=jnp.float32
    )
    return partial_value + lax.dot_general(
        grad_up, wup, contract_cols, preferred_element_type=jnp.float32
    )


def row_sum(left, right):
    return lax.dot_general(
        left, right, (((0,), (0,)), ((), ())), preferred_element_type=jnp.float32
    )


def on_device(
    tokens, grad_out, expert_ids, gate_weights, gate_codes, up_codes, down_codes, block_scales
):
    experts = lax.axis_size("eg")
    width = tokens.shape[1]
    capacity = 2 * tokens.shape[0] * TOPK // experts
    placed, picked = routing_tables(expert_ids, experts, capacity)
    placed_low = placed.astype(jnp.bfloat16)
    send_tokens = jnp.einsum(
        "tec,td->ecd", placed_low, tokens, preferred_element_type=jnp.float32
    ).astype(jnp.bfloat16)
    send_cotan = jnp.einsum(
        "tec,td->ecd", placed_low, grad_out, preferred_element_type=jnp.float32
    ).astype(jnp.bfloat16)
    send_gates = jnp.einsum(
        "tkec,tk->ec", picked, gate_weights.astype(jnp.float32), precision=lax.Precision.HIGHEST
    ).astype(jnp.bfloat16)
    recv_tokens, recv_cotan, recv_gates = (
        lax.all_to_all(send_tokens, "eg", split_axis=0, concat_axis=0, tiled=True),
        lax.all_to_all(send_cotan, "eg", split_axis=0, concat_axis=0, tiled=True),
        lax.all_to_all(send_gates, "eg", split_axis=0, concat_axis=0, tiled=True),
    )
    wgate = dequantize(gate_codes[0], block_scales[0, 0])
    wup = dequantize(up_codes[0], block_scales[0, 1])
    wdown = dequantize(down_codes[0], block_scales[0, 2])
    all_tokens, all_cotan, all_gates = (
        lax.all_gather(recv_tokens, "blk", axis=0, tiled=True),
        lax.all_gather(recv_cotan, "blk", axis=0, tiled=True),
        lax.all_gather(recv_gates, "blk", axis=0, tiled=True),
    )
    feats = all_tokens.reshape(-1, width)
    cotan = all_cotan.reshape(-1, width)
    gates = all_gates.reshape(-1).astype(jnp.float32)
    gate_pre = jnp.dot(feats, wgate, preferred_element_type=jnp.float32)
    up_pre = jnp.dot(feats, wup, preferred_element_type=jnp.float32)
    down_back = jnp.dot(cotan, wdown, preferred_element_type=jnp.float32)
    hidden, grad_gate, grad_up, gated_hidden = backward_math(gate_pre, up_pre, down_back, gates)
    contrib = project_back(grad_gate, grad_up, wgate, wup)
    scores = jnp.sum(hidden * down_back, axis=1)
    contrib, scores, grad_gate, grad_up, gated_hidden, feats, cotan = (
        contrib,
        scores,
        grad_gate,
        grad_up,
        gated_hidden,
        feats,
        cotan,
    )
    slots = contrib.shape[0] // capacity
    summed_rows, summed_scores = (
        lax.psum_scatter(
            contrib.reshape(slots, capacity, width).astype(jnp.bfloat16),
            "blk",
            scatter_dimension=0,
            tiled=True,
        ).astype(jnp.float32),
        lax.psum_scatter(
            scores.reshape(slots, capacity).astype(jnp.bfloat16),
            "blk",
            scatter_dimension=0,
            tiled=True,
        ).astype(jnp.float32),
    )
    back_rows = summed_rows.astype(jnp.bfloat16)
    back_gates = summed_scores.astype(jnp.bfloat16)
    gate_grad = row_sum(feats, grad_gate).astype(jnp.bfloat16)[None]
    up_grad = row_sum(feats, grad_up).astype(jnp.bfloat16)[None]
    down_grad = row_sum(cotan, gated_hidden).astype(jnp.bfloat16)[None]
    home_rows, home_gates = (
        lax.all_to_all(back_rows, "eg", split_axis=0, concat_axis=0, tiled=True),
        lax.all_to_all(back_gates, "eg", split_axis=0, concat_axis=0, tiled=True),
    )
    grad_tokens = jnp.einsum(
        "tec,ecd->td", placed_low, home_rows, preferred_element_type=jnp.float32
    ).astype(jnp.bfloat16)
    grad_gates = jnp.einsum(
        "tkec,ec->tk", picked, home_gates.astype(jnp.float32), precision=lax.Precision.HIGHEST
    ).astype(jnp.bfloat16)
    return (grad_tokens, grad_gates, gate_grad, up_grad, down_grad)


def solution(mesh):
    in_specs = (
        P(("eg", "blk"), None),
        P(("eg", "blk"), None),
        P(("eg", "blk"), None),
        P(("eg", "blk"), None),
        P("eg", None, "blk"),
        P("eg", None, "blk"),
        P("eg", None, "blk"),
        P("eg", None, "blk", None),
    )
    out_specs = (
        P(("eg", "blk"), None),
        P(("eg", "blk"), None),
        P("eg", None, "blk"),
        P("eg", None, "blk"),
        P("eg", None, "blk"),
    )
    return jax.shard_map(
        on_device, mesh=mesh, in_specs=in_specs, out_specs=out_specs, check_vma=False
    )
```

profile of v0, /device:TPU:32, one launch (start us, length us, event | category | flops | bytes accessed | tf_op | source)
XLA Modules:
  0.0 404.0 jit_solution(2032406847391941953)
XLA Ops:
  7.3 0.8 fusion.42
  8.1 0.3 convolution_convert_fusion.3
  8.4 0.5 copy.45
  8.9 26.1 %all_to_all.39 = bf16[16,2,7168]{2,1,0:T(2,128)(2,1)} all-to-all(bf16[16,2,7168]{2,1,0:T(2,128)(2,1)S(1)} %copy.45), channel_id=1, replica_groups=mesh['eg'=16,'blk'=16] {'eg'}, dimensions={0} | all-to-all | bytes 917504 | tf_op jit(solution)/shard_map/all_to_all | solution.py:77
  35.0 0.0 all-gather.4.cloned.1.call-start
  35.1 1.2 convolution_convert_fusion.4
  36.3 0.5 copy.44
  36.8 19.8 %all_to_all.40 = bf16[16,2,7168]{2,1,0:T(2,128)(2,1)} all-to-all(bf16[16,2,7168]{2,1,0:T(2,128)(2,1)S(1)} %copy.44), channel_id=1, replica_groups=mesh['eg'=16,'blk'=16] {'eg'}, dimensions={0} | all-to-all | bytes 917504 | tf_op jit(solution)/shard_map/all_to_all | solution.py:78
  56.6 0.1 copy.69
  56.7 0.1 fusion.32
  56.7 0.1 copy.42
  56.9 0.1 multiply_reduce_fusion.2
  57.0 0.1 copy.73
  57.1 0.7 copy.43
  57.8 5.4 %all-to-all-start = ((bf16[16,1,2]{2,1,0:T(2,128)(2,1)}), bf16[16,1,2]{2,1,0:T(2,128)(2,1)S(1)}, u32[]{:S(2)}, u32[]{:S(2)}) async-start(bf16[16,1,2]{2,1,0:T(2,128)(2,1)} %copy.43), calls=%async_computation | async-start | bytes 16384 | tf_op jit(solution)/shard_map/all_to_all | solution.py:79
  63.2 0.1 broadcast_bitcast_fusion
  63.3 0.1 broadcast_bitcast_fusion.2
  63.4 8.4 %all-to-all-done = bf16[16,1,2]{2,1,0:T(2,128)(2,1)S(1)} async-done(((bf16[16,1,2]{2,1,0:T(2,128)(2,1)}), bf16[16,1,2]{2,1,0:T(2,128)(2,1)S(1)}, u32[]{:S(2)}, u32[]{:S(2)}) %all-to-all-start) | async-done | bytes 96 | tf_op jit(solution)/shard_map/all_to_all | solution.py:79
  71.7 20.1 %all-gather = bf16[256,1,2]{2,1,0:T(2,128)(2,1)S(1)} all-gather(bf16[16,1,2]{2,1,0:T(2,128)(2,1)S(1)} %all-to-all-done), channel_id=2, replica_groups=mesh['eg'=16,'blk'=16] {'blk'}, dimensions={0}, use_global_device_ids=true | all-gather | bytes 1088 | tf_op jit(solution)/shard_map/all_gather | solution.py:87
  91.8 0.4 convert_reduce_fusion
  92.2 0.1 reshape.141
  92.4 15.6 %reshape.140 = bf16[512,7168]{1,0:T(8,128)(2,1)} reshape(bf16[256,2,7168]{2,1,0:T(2,128)(2,1)} %all-gather.6.cloned.1.call-done) | data formatting | bytes 14680064 | tf_op jit(solution)/shard_map/reshape | solution.py:89
  108.0 7.5 %fusion.16 = f32[512,128]{0,1:T(8,128)S(1)} fusion(bf16[512,7168]{1,0:T(8,128)(2,1)} %reshape.140, bf16[1,7168,128]{2,1,0:T(8,128)(2,1)S(1)} %copy-done.3, f32[7168]{0:T(1024)S(1)} %get-tuple-element.11), kind=kOutput, calls=%fused_computation.26 | convolution fusion | flops 942276608 | bytes 9465856 | tf_op jit(solution)/shard_map/dot_general | solution.py:92
  115.5 2.9 fusion.20
  118.4 19.6 %all-gather.4.cloned.1.call-done = bf16[256,2,7168]{2,1,0:T(2,128)(2,1)} async-done(((bf16[16,2,7168]{2,1,0:T(2,128)(2,1)}), bf16[256,2,7168]{2,1,0:T(2,128)(2,1)}) %all-gather.4.cloned.1.call-update) | async-done | bytes 7340048 | tf_op jit(solution)/shard_map/all_gather | solution.py:86
  138.0 15.4 %reshape.139 = bf16[512,7168]{1,0:T(8,128)(2,1)} reshape(bf16[256,2,7168]{2,1,0:T(2,128)(2,1)} %all-gather.4.cloned.1.call-done) | data formatting | bytes 14680064 | tf_op jit(solution)/shard_map/reshape | solution.py:90
  153.4 6.6 %multiply_reduce_fusion = (bf16[512]{0:T(512)(128)(2,1)S(1)}, bf16[512,128]{0,1:T(8,128)(2,1)S(1)}, bf16[512,128]{0,1:T(8,128)(2,1)S(1)}) fusion(f32[512,128]{0,1:T(8,128)S(1)} %fusion.20, f32[512,128]{0,1:T(8,128)S(1)} %fusion.16, f32[512]{0:T(512)S(1)} %reshape.141, bf16[512,7168]{1,0:T(8,128)(2,1)} %reshape.139, bf16[1,7168,128]{2,1,0:T(8,128)(2,1)} %param.14, ...), kind=kOutput, calls=%fused_computation.36 | convolution fusion | flops 943455744 | bytes 9993216 | tf_op jit(solution)/shard_map/dot_general | solution.py:94
  160.0 0.8 convert_element_type.210
  160.9 0.3 all-reduce.3.cloned.1.call-start
  161.2 4.8 %fusion.13 = f32[512,7168]{1,0:T(8,128)S(1)} fusion(bf16[512,128]{0,1:T(8,128)(2,1)S(1)} %get-tuple-element.6, bf16[1,7168,128]{2,1,0:T(8,128)(2,1)S(1)} %copy-done.3, f32[7168]{0:T(1024)S(1)} %get-tuple-element.11), kind=kOutput, calls=%fused_computation.24 | convolution fusion | flops 942276608 | bytes 16674816 | tf_op jit(solution)/shard_map/dot_general | solution.py:45
  166.0 5.9 %add_convert_fusion = bf16[512,7168]{1,0:T(8,128)(2,1)} fusion(f32[512,7168]{1,0:T(8,128)S(1)} %fusion.13, bf16[512,128]{0,1:T(8,128)(2,1)S(1)} %get-tuple-element.7, bf16[1,7168,128]{2,1,0:T(8,128)(2,1)S(1)} %copy-done.5, f32[7168]{0:T(1024)S(1)} %get-tuple-element.12), kind=kOutput, calls=%fused_computation | convolution fusion | flops 949616640 | bytes 24014848 | tf_op jit(solution)/shard_map/dot_general | solution.py:48
  171.9 14.9 %convert_element_type.207 = bf16[256,2,7168]{2,1,0:T(2,128)(2,1)} reshape(bf16[512,7168]{1,0:T(8,128)(2,1)} %add_convert_fusion) | data formatting | bytes 14680064 | tf_op jit(solution)/shard_map/convert_element_type | solution.py:110
  186.8 0.6 copy-done.9
  187.5 0.6 dynamic-slice
  188.7 6.5 %fusion.2 = bf16[1,7168,128]{2,1,0:T(8,128)(2,1)} fusion(bf16[512,7168]{1,0:T(8,128)(2,1)} %reshape.139, f32[512]{0:T(512)S(1)} %reshape.141, f32[512,128]{0,1:T(8,128)S(1)} %fusion.20, f32[512,128]{0,1:T(8,128)S(1)} %fusion.16), kind=kOutput, calls=%fused_computation.6 | convolution fusion | flops 940900352 | bytes 9701376 | tf_op jit(solution)/shard_map/dot_general | solution.py:54
  195.2 30.4 %reduce-scatter.2.cloned.1.call-done = bf16[16,2]{1,0:T(8,128)(2,1)} async-done(((bf16[256,2]{1,0:T(8,128)(2,1)}), bf16[16,2]{1,0:T(8,128)(2,1)}) %reduce-scatter.2.cloned.1.call-update) | async-done | bytes 80 | tf_op jit(solution)/shard_map/reduce_scatter | solution.py:115
  225.6 1.3 copy.48
  226.9 9.4 %all-to-all-start.4 = ((bf16[16,1,2]{2,1,0:T(2,128)(2,1)}), bf16[16,1,2]{2,1,0:T(2,128)(2,1)S(1)}, u32[]{:S(2)}, u32[]{:S(2)}) async-start(bf16[16,1,2]{2,1,0:T(2,128)(2,1)} %copy.48), calls=%async_computation.5 | async-start | bytes 16384 | tf_op jit(solution)/shard_map/all_to_all | solution.py:129
  236.3 134.6 %all-reduce.3.cloned.1.call-done = bf16[256,2,7168]{2,1,0:T(2,128)(2,1)} async-done(((bf16[256,2,7168]{2,1,0:T(2,128)(2,1)}), bf16[256,2,7168]{2,1,0:T(2,128)(2,1)}) %all-reduce.3.cloned.1.call-update) | async-done | bytes 7340048
  370.9 2.1 constant_dynamic-slice_fusion
  373.0 9.6 %all-to-all-start.3 = ((bf16[16,2,7168]{2,1,0:T(2,128)(2,1)}), bf16[16,2,7168]{2,1,0:T(2,128)(2,1)S(1)}, u32[]{:S(2)}, u32[]{:S(2)}) async-start(bf16[16,2,7168]{2,1,0:T(2,128)(2,1)} %constant_dynamic-slice_fusion), calls=%async_computation.3 | async-start | bytes 917504 | tf_op jit(solution)/shard_map/all_to_all | solution.py:128
  382.7 6.5 %fusion = bf16[1,7168,128]{2,1,0:T(8,128)(2,1)} fusion(bf16[512,7168]{1,0:T(8,128)(2,1)} %reshape.140, bf16[512,128]{0,1:T(8,128)(2,1)S(1)} %get-tuple-element.6), kind=kOutput, calls=%fused_computation.4 | convolution fusion | flops 940441600 | bytes 9306112 | tf_op jit(solution)/shard_map/dot_general | solution.py:54
  389.1 6.4 %fusion.1 = bf16[1,7168,128]{2,1,0:T(8,128)(2,1)} fusion(bf16[512,7168]{1,0:T(8,128)(2,1)} %reshape.140, bf16[512,128]{0,1:T(8,128)(2,1)S(1)} %get-tuple-element.7), kind=kOutput, calls=%fused_computation.5 | convolution fusion | flops 940441600 | bytes 9306112 | tf_op jit(solution)/shard_map/dot_general | solution.py:54
  395.6 0.1 copy.68
  395.7 0.1 copy.70
  395.8 0.2 multiply_reduce_fusion.1
  396.0 0.6 copy.65
  396.6 0.9 fusion.3
  (35 shorter events, 0.3 us)
Async XLA Ops:
  7.2 0.9 copy-start
  7.2 49.5 %copy-start.6 = (s32[8,2]{0,1:T(2,128)S(1)}, s32[8,2]{0,1:T(2,128)}, u32[]{:S(2)}) copy-start(s32[8,2]{0,1:T(2,128)} %param.10) | copy-start | bytes 196
  7.2 49.4 %copy-start.8 = (bf16[8,2]{0,1:T(2,128)(2,1)S(1)}, bf16[8,2]{0,1:T(2,128)(2,1)}, u32[]{:S(2)}) copy-start(bf16[8,2]{0,1:T(2,128)(2,1)} %param.11) | copy-start | bytes 100
  7.2 56.0 %copy-start.7 = (bf16[1,3,1,56]{3,1,2,0:T(4,128)(2,1)S(1)}, bf16[1,3,1,56]{3,1,2,0:T(4,128)(2,1)}, u32[]{:S(2)}) copy-start(bf16[1,3,1,56]{3,1,2,0:T(4,128)(2,1)} %param.15) | copy-start | bytes 1012
  7.2 85.1 %all-gather.6.cloned.1.call-start = ((), (), s32[]{:S(2)}) async-start(), calls=%async_computation.7 | async-start | bytes 7798784 | tf_op jit(solution)/shard_map/all_gather | solution.py:85
  35.0 103.0 %all-gather.4.cloned.1.call-start = ((), (), s32[]{:S(2)}) async-start(), calls=%async_computation.6 | async-start | bytes 7798784 | tf_op jit(solution)/shard_map/all_gather | solution.py:86
  57.8 13.9 %all-to-all-start = ((bf16[16,1,2]{2,1,0:T(2,128)(2,1)}), bf16[16,1,2]{2,1,0:T(2,128)(2,1)S(1)}, u32[]{:S(2)}, u32[]{:S(2)}) async-start(bf16[16,1,2]{2,1,0:T(2,128)(2,1)} %copy.43), calls=%async_computation | async-start | bytes 16384 | tf_op jit(solution)/shard_map/all_to_all | solution.py:79
  63.2 162.4 %reduce-scatter.2.cloned.1.call-start = ((), (), s32[]{:S(2)}) async-start(), calls=%async_computation.8 | async-start | bytes 69632 | tf_op jit(solution)/shard_map/reduce_scatter | solution.py:115
  92.3 15.6 %copy-start.3 = (bf16[1,7168,128]{2,1,0:T(8,128)(2,1)S(1)}, bf16[1,7168,128]{2,1,0:T(8,128)(2,1)}, u32[]{:S(2)}) copy-start(bf16[1,7168,128]{2,1,0:T(8,128)(2,1)} %param.12) | copy-start | bytes 5505028
  108.0 7.5 %copy-start.2 = (bf16[512,7168]{1,0:T(8,128)(2,1)S(1)}, bf16[512,7168]{1,0:T(8,128)(2,1)}, u32[]{:S(2)}) copy-start(bf16[512,7168]{1,0:T(8,128)(2,1)} %reshape.140) | copy-start | bytes 22020100
  108.0 7.5 %copy-start.4 = (bf16[1,7168,128]{2,1,0:T(8,128)(2,1)S(1)}, bf16[1,7168,128]{2,1,0:T(8,128)(2,1)}, u32[]{:S(2)}) copy-start(bf16[1,7168,128]{2,1,0:T(8,128)(2,1)} %param.13) | copy-start | bytes 5505028
  160.9 210.1 %all-reduce.3.cloned.1.call-start = ((), (), s32[]{:S(2)}) async-start(), calls=%async_computation.9 | async-start | bytes 14680064
  161.1 4.8 %copy-start.5 = (bf16[1,7168,128]{2,1,0:T(8,128)(2,1)S(1)}, bf16[1,7168,128]{2,1,0:T(8,128)(2,1)}, u32[]{:S(2)}) copy-start(bf16[1,7168,128]{2,1,0:T(8,128)(2,1)} %param.13) | copy-start | bytes 5505028
  186.8 0.7 copy-start.9
  226.9 146.2 %all-to-all-start.4 = ((bf16[16,1,2]{2,1,0:T(2,128)(2,1)}), bf16[16,1,2]{2,1,0:T(2,128)(2,1)S(1)}, u32[]{:S(2)}, u32[]{:S(2)}) async-start(bf16[16,1,2]{2,1,0:T(2,128)(2,1)} %copy.48), calls=%async_computation.5 | async-start | bytes 16384 | tf_op jit(solution)/shard_map/all_to_all | solution.py:129
  373.0 23.5 %all-to-all-start.3 = ((bf16[16,2,7168]{2,1,0:T(2,128)(2,1)}), bf16[16,2,7168]{2,1,0:T(2,128)(2,1)S(1)}, u32[]{:S(2)}, u32[]{:S(2)}) async-start(bf16[16,2,7168]{2,1,0:T(2,128)(2,1)} %constant_dynamic-slice_fusion), calls=%async_computation.3 | async-start | bytes 917504 | tf_op jit(solution)/shard_map/all_to_all | solution.py:128
  382.6 14.8 %copy-start.1 = (bf16[8,7168]{1,0:T(8,128)(2,1)S(1)}, bf16[8,7168]{1,0:T(8,128)(2,1)}, u32[]{:S(2)}) copy-start(bf16[8,7168]{1,0:T(8,128)(2,1)} %param.8) | copy-start | bytes 344068
Sparse Core Ops, SparseCore 0:
  35.1 50.4 all-gather.5
  87.5 50.5 all-gather.3
  161.0 64.5 reduce-scatter.1
  228.1 142.7 all-reduce.2
where the time goes:
time: 406 us; the launch traced here: 404 us
  waiting for transfers between devices  193 us (48%)
  blocking collectives  65.9 us (16%)
  local copies, waits for them, and re-layouts  54.4 us (13%)
  matrix products  49.6 us (12%)
  starting transfers between devices  24.8 us (6%)
  between operations  14.6 us (4%)
    unnamed x5, waiting for transfers between devices  135 us
    reduce_scatter x1, waiting for transfers between devices, on_device(): lax.psum_scatter(scores.reshape(slots, capacity).astype(jnp.bfloat16), 'b...  30.4 us
    all_to_all x1, blocking collectives, on_device(): lax.all_to_all(send_tokens, 'eg', split_axis=0, concat_axis=0, tiled=True)  26.1 us
    all_gather x1, blocking collectives, on_device(): lax.all_gather(recv_gates, 'blk', axis=0, tiled=True)  20.1 us
    all_to_all x1, blocking collectives, on_device(): lax.all_to_all(send_cotan, 'eg', split_axis=0, concat_axis=0, tiled=True)  19.8 us
    all_gather x1, waiting for transfers between devices, on_device(): lax.all_gather(recv_cotan, 'blk', axis=0, tiled=True)  19.6 us
    dot_general x3, matrix products, row_sum(): lax.dot_general(left, right, (((0,), (0,)), ((), ())), preferred_element_...  19.4 us
    reshape x1, local copies, waits for them, and re-layouts, on_device(): feats = all_tokens.reshape(-1, width)  15.6 us
  transfers between devices with their start and end apart: 7, of which 4 were waited for; matrix products, arithmetic and copies ran while one was open for 20% of the time, Pallas kernels for 0%

commit v1 on v0

--- a/solution.py
+++ b/solution.py
@@ -5,6 +5,7 @@
 
 QBLOCK = 128
 TOPK = 2
+LANE = 128
 
 
 def dequantize(codes, scales):
@@ -64,75 +65,46 @@
     capacity = 2 * tokens.shape[0] * TOPK // experts
     placed, picked = routing_tables(expert_ids, experts, capacity)
     placed_low = placed.astype(jnp.bfloat16)
-    send_tokens = jnp.einsum(
-        "tec,td->ecd", placed_low, tokens, preferred_element_type=jnp.float32
-    ).astype(jnp.bfloat16)
-    send_cotan = jnp.einsum(
-        "tec,td->ecd", placed_low, grad_out, preferred_element_type=jnp.float32
+    both = jnp.concatenate([tokens, grad_out], axis=1)
+    send_rows = jnp.einsum(
+        "tec,td->ecd", placed_low, both, preferred_element_type=jnp.float32
     ).astype(jnp.bfloat16)
     send_gates = jnp.einsum(
         "tkec,tk->ec", picked, gate_weights.astype(jnp.float32), precision=lax.Precision.HIGHEST
     ).astype(jnp.bfloat16)
-    recv_tokens, recv_cotan, recv_gates = (
-        lax.all_to_all(send_tokens, "eg", split_axis=0, concat_axis=0, tiled=True),
-        lax.all_to_all(send_cotan, "eg", split_axis=0, concat_axis=0, tiled=True),
-        lax.all_to_all(send_gates, "eg", split_axis=0, concat_axis=0, tiled=True),
-    )
+    gate_block = jnp.pad(send_gates[:, :, None], ((0, 0), (0, 0), (0, LANE - 1)))
+    send = jnp.concatenate([send_rows, gate_block], axis=2)
+    recv = lax.all_to_all(send, "eg", split_axis=0, concat_axis=0, tiled=True)
+    recv = recv.reshape(experts * capacity, recv.shape[2])
     wgate = dequantize(gate_codes[0], block_scales[0, 0])
     wup = dequantize(up_codes[0], block_scales[0, 1])
     wdown = dequantize(down_codes[0], block_scales[0, 2])
-    all_tokens, all_cotan, all_gates = (
-        lax.all_gather(recv_tokens, "blk", axis=0, tiled=True),
-        lax.all_gather(recv_cotan, "blk", axis=0, tiled=True),
-        lax.all_gather(recv_gates, "blk", axis=0, tiled=True),
-    )
-    feats = all_tokens.reshape(-1, width)
-    cotan = all_cotan.reshape(-1, width)
-    gates = all_gates.reshape(-1).astype(jnp.float32)
+    gathered = lax.all_gather(recv, "blk", axis=0, tiled=True)
+    feats = gathered[:, :width]
+    cotan = gathered[:, width : 2 * width]
+    gates = gathered[:, 2 * width].astype(jnp.float32)
     gate_pre = jnp.dot(feats, wgate, preferred_element_type=jnp.float32)
     up_pre = jnp.dot(feats, wup, preferred_element_type=jnp.float32)
     down_back = jnp.dot(cotan, wdown, preferred_element_type=jnp.float32)
     hidden, grad_gate, grad_up, gated_hidden = backward_math(gate_pre, up_pre, down_back, gates)
-    contrib = project_back(grad_gate, grad_up, wgate, wup)
-    scores = jnp.sum(hidden * down_back, axis=1)
-    contrib, scores, grad_gate, grad_up, gated_hidden, feats, cotan = (
-        contrib,
-        scores,
-        grad_gate,
-        grad_up,
-        gated_hidden,
-        feats,
-        cotan,
-    )
-    slots = contrib.shape[0] // capacity
-    summed_rows, summed_scores = (
-        lax.psum_scatter(
-            contrib.reshape(slots, capacity, width).astype(jnp.bfloat16),
-            "blk",
-            scatter_dimension=0,
-            tiled=True,
-        ).astype(jnp.float32),
-        lax.psum_scatter(
-            scores.reshape(slots, capacity).astype(jnp.bfloat16),
-            "blk",
-            scatter_dimension=0,
-            tiled=True,
-        ).astype(jnp.float32),
-    )
-    back_rows = summed_rows.astype(jnp.bfloat16)
-    back_gates = summed_scores.astype(jnp.bfloat16)
+    contrib = project_back(grad_gate, grad_up, wgate, wup).astype(jnp.bfloat16)
+    scores = jnp.sum(hidden * down_back, axis=1).astype(jnp.bfloat16)
+    score_block = jnp.pad(scores[:, None], ((0, 0), (0, LANE - 1)))
+    partial_rows = jnp.concatenate([contrib, score_block], axis=1)
+    summed = lax.psum_scatter(partial_rows, "blk", scatter_dimension=0, tiled=True)
     gate_grad = row_sum(feats, grad_gate).astype(jnp.bfloat16)[None]
     up_grad = row_sum(feats, grad_up).astype(jnp.bfloat16)[None]
     down_grad = row_sum(cotan, gated_hidden).astype(jnp.bfloat16)[None]
-    home_rows, home_gates = (
-        lax.all_to_all(back_rows, "eg", split_axis=0, concat_axis=0, tiled=True),
-        lax.all_to_all(back_gates, "eg", split_axis=0, concat_axis=0, tiled=True),
-    )
+    summed = summed.reshape(experts, capacity, summed.shape[1])
+    home = lax.all_to_all(summed, "eg", split_axis=0, concat_axis=0, tiled=True)
     grad_tokens = jnp.einsum(
-        "tec,ecd->td", placed_low, home_rows, preferred_element_type=jnp.float32
+        "tec,ecd->td", placed_low, home[:, :, :width], preferred_element_type=jnp.float32
     ).astype(jnp.bfloat16)
     grad_gates = jnp.einsum(
-        "tkec,ec->tk", picked, home_gates.astype(jnp.float32), precision=lax.Precision.HIGHEST
+        "tkec,ec->tk",
+        picked,
+        home[:, :, width].astype(jnp.float32),
+        precision=lax.Precision.HIGHEST,
     ).astype(jnp.bfloat16)
     return (grad_tokens, grad_gates, gate_grad, up_grad, down_grad)
 

time: 406 us -> 282 us (0.69)
  local copies, waits for them, and re-layouts: 54.4 us -> 5.8 us
  waiting for transfers between devices: 193 us -> 152 us
  blocking collectives: 65.9 us -> 36.3 us
  starting transfers between devices: 24.8 us -> 9.84 us
  other arithmetic: 1.58 us -> 10.2 us
    unnamed x5 -> x2, waiting for transfers between devices: 135 us -> 0.03 us
    all_gather x2 -> x1, waiting for transfers between devices: 19.6 us -> 81.2 us  [on_device(): gathered = lax.all_gather(recv, 'blk', axis=0, tiled=True)]
    reduce_scatter x1, waiting for transfers between devices: 30.4 us -> 70.5 us  [on_device(): lax.psum_scatter(partial_rows, 'blk', scatter_dimension=0, tiled=True)]
    reshape x2, local copies, waits for them, and re-layouts: 31 us -> 3.25 us  [the longest x1 1.98 us: on_device(): summed = summed.reshape(experts, capacity, summed.shape[1])]
    all_gather x1 -> x0, blocking collectives: 20.1 us -> none  [on_device(): lax.all_gather(recv_gates, 'blk', axis=0, tiled=True)]
    convert_element_type x5 -> x1, local copies, waits for them, and re-layouts: 16.8 us -> 0.13 us  [on_device(): scores = jnp.sum(hidden * down_back, axis=1).astype(jnp.bfloat16)]
    all_to_all x3 -> x1, starting transfers between devices: 24.4 us -> 9.76 us  [on_device(): home = lax.all_to_all(summed, 'eg', split_axis=0, concat_axis=0, tiled=True)]
    all_to_all x2 -> x1, blocking collectives: 45.9 us -> 36.3 us  [on_device(): recv = lax.all_to_all(send, 'eg', split_axis=0, concat_axis=0, tiled=True)]
  transfers between devices with their start and end apart: 7 -> 3, of which waited for: 4 -> 2; matrix products, arithmetic and copies ran while one was open for 20% -> 7% of each run, Pallas kernels for 0% -> 0%
where the time goes in v1:
time: 282 us; the launch traced here: 281 us
  waiting for transfers between devices  152 us (54%)
  matrix products  52.7 us (19%)
  blocking collectives  36.3 us (13%)
  between operations  14.2 us (5%)
  other arithmetic  10.2 us (4%)
  starting transfers between devices  9.84 us (3%)
  local copies, waits for them, and re-layouts  5.8 us (2%)
    all_gather x1, waiting for transfers between devices, on_device(): gathered = lax.all_gather(recv, 'blk', axis=0, tiled=True)  81.2 us
    reduce_scatter x1, waiting for transfers between devices, on_device(): lax.psum_scatter(partial_rows, 'blk', scatter_dimension=0, tiled=True)  70.5 us
    all_to_all x1, blocking collectives, on_device(): recv = lax.all_to_all(send, 'eg', split_axis=0, concat_axis=0, tiled=True)  36.3 us
    dot_general x3, matrix products, row_sum(): lax.dot_general(left, right, (((0,), (0,)), ((), ())), preferred_element_...  19.4 us
    all_to_all x1, starting transfers between devices, on_device(): home = lax.all_to_all(summed, 'eg', split_axis=0, concat_axis=0, tiled=True)  9.76 us
    dot_general x1, matrix products, on_device(): gate_pre = jnp.dot(feats, wgate, preferred_element_type=jnp.float32)  6.82 us
    dot_general x1, matrix products, on_device(): up_pre = jnp.dot(feats, wup, preferred_element_type=jnp.float32)  6.78 us
    dot_general x1, matrix products, on_device(): down_back = jnp.dot(cotan, wdown, preferred_element_type=jnp.float32)  6.78 us
  transfers between devices with their start and end apart: 3, of which 2 were waited for; matrix products, arithmetic and copies ran while one was open for 7% of the time, Pallas kernels for 0%

profile of v1, /device:TPU:32, one launch (start us, length us, event | category | flops | bytes accessed | tf_op | source)
XLA Modules:
  0.0 280.8 jit_solution(11219898954666444292)
XLA Ops:
  7.2 0.0 all-gather.2.cloned.1.call-start
  7.2 0.8 fusion.40
  8.0 0.7 fusion.33
  8.7 0.7 bitcast_convert_fusion.4
  9.4 0.1 copy.55
  9.5 0.1 copy.31
  9.6 0.1 multiply_reduce_fusion.2
  9.8 0.1 copy.59
  9.8 0.1 copy.32
  10.0 1.4 convolution_convert_fusion
  11.4 0.1 fusion.22
  11.4 0.0 copy-start.2
  11.4 0.0 copy-start.3
  11.5 0.7 copy.33
  12.2 36.3 %all_to_all.10 = bf16[16,2,14464]{2,1,0:T(2,128)(2,1)S(1)} all-to-all(bf16[16,2,14464]{2,1,0:T(2,128)(2,1)S(1)} %copy.33), channel_id=1, replica_groups=mesh['eg'=16,'blk'=16] {'eg'}, dimensions={0} | all-to-all | bytes 1851392 | tf_op jit(solution)/shard_map/all_to_all | solution.py:77
  48.5 1.3 reshape.109
  49.8 0.0 all-gather.2.cloned.1.call-update
  49.8 0.0 reduce-scatter.2.cloned.1.call-start
  49.8 0.0 copy-done.2
  49.9 0.1 broadcast_bitcast_fusion.2
  49.9 0.1 broadcast_bitcast_fusion
  50.0 81.2 %all-gather.2.cloned.1.call-done = bf16[512,14464]{1,0:T(8,128)(2,1)} async-done(((bf16[32,14464]{1,0:T(8,128)(2,1)}), bf16[512,14464]{1,0:T(8,128)(2,1)}) %all-gather.2.cloned.1.call-update) | async-done | bytes 14811152 | tf_op jit(solution)/shard_map/all_gather | solution.py:82
  131.2 1.0 convert_reduce_fusion
  132.2 0.0 copy-done.3
  132.2 0.0 copy-start.1
  132.3 6.8 %fusion.7 = f32[512,128]{0,1:T(8,128)S(1)} fusion(bf16[512,14464]{1,0:T(8,128)(2,1)} %all-gather.2.cloned.1.call-done, bf16[1,7168,128]{2,1,0:T(8,128)(2,1)S(1)} %copy-done.3, f32[7168]{0:T(1024)S(1)} %broadcast_bitcast_fusion.2), kind=kOutput, calls=%fused_computation.14 | convolution fusion | flops 942276608 | bytes 9465856 | tf_op jit(solution)/shard_map/dot_general | solution.py:88
  139.0 0.0 copy-done.1
  139.0 0.0 copy-start
  139.1 6.8 %fusion.13 = f32[512,128]{0,1:T(8,128)S(1)} fusion(bf16[512,14464]{1,0:T(8,128)(2,1)} %all-gather.2.cloned.1.call-done, bf16[1,7168,128]{2,1,0:T(8,128)(2,1)S(1)} %copy-done.1, f32[7168]{0:T(1024)S(1)} %get-tuple-element.13), kind=kOutput, calls=%fused_computation.20 | convolution fusion | flops 942276608 | bytes 9465856 | tf_op jit(solution)/shard_map/dot_general | solution.py:87
  145.9 6.8 %multiply_convert_fusion.2 = (bf16[512,128]{0,1:T(8,128)(2,1)S(1)}, bf16[512]{0:T(512)(128)(2,1)S(1)}, bf16[512,128]{0,1:T(8,128)(2,1)S(1)}, f32[512,128]{0,1:T(8,128)S(1)}) fusion(f32[512,128]{0,1:T(8,128)S(1)} %fusion.13, f32[512,128]{0,1:T(8,128)S(1)} %fusion.7, f32[512]{0:T(512)S(1)} %convert_reduce_fusion, bf16[1,7168,128]{2,1,0:T(8,128)(2,1)S(1)} %copy-done, ...), kind=kOutput, calls=%fused_computation.40 | convolution fusion | flops 943455744 | bytes 10255360 | tf_op jit(solution)/shard_map/dot_general | solution.py:86
  152.7 0.1 convert_element_type.188
  152.8 4.8 %fusion.25 = f32[512,7168]{1,0:T(8,128)S(1)} fusion(bf16[512,128]{0,1:T(8,128)(2,1)S(1)} %get-tuple-element.5, bf16[1,7168,128]{2,1,0:T(8,128)(2,1)S(1)} %copy-done, f32[7168]{0:T(1024)S(1)} %get-tuple-element.12), kind=kOutput, calls=%fused_computation.33 | convolution fusion | flops 942276608 | bytes 16674816 | tf_op jit(solution)/shard_map/dot_general | solution.py:46
  157.6 5.9 %add_convert_fusion = bf16[512,7168]{1,0:T(8,128)(2,1)} fusion(f32[512,7168]{1,0:T(8,128)S(1)} %fusion.25, bf16[512,128]{0,1:T(8,128)(2,1)S(1)} %get-tuple-element.7, bf16[1,7168,128]{2,1,0:T(8,128)(2,1)S(1)} %copy-done.1, f32[7168]{0:T(1024)S(1)} %get-tuple-element.13), kind=kOutput, calls=%fused_computation.3 | convolution fusion | flops 949616640 | bytes 24014848 | tf_op jit(solution)/shard_map/dot_general | solution.py:49
  163.5 6.6 %fusion.5 = bf16[512,7296]{1,0:T(8,128)(2,1)} fusion(bf16[512,1]{1,0:T(8,128)(2,1)S(1)} %convert_element_type.188, bf16[512,7168]{1,0:T(8,128)(2,1)} %add_convert_fusion), kind=kLoop, calls=%fused_computation.12 | loop fusion | flops 22413312 | bytes 14812160 | tf_op jit(solution)/shard_map/concatenate | solution.py:93
  170.1 0.0 reduce-scatter.2.cloned.1.call-update
  170.1 6.4 %fusion.1 = bf16[1,7168,128]{2,1,0:T(8,128)(2,1)} fusion(bf16[512,128]{0,1:T(8,128)(2,1)S(1)} %get-tuple-element.5, bf16[512,14464]{1,0:T(8,128)(2,1)} %all-gather.2.cloned.1.call-done), kind=kOutput, calls=%fused_computation.7 | convolution fusion | flops 940441600 | bytes 9306112 | tf_op jit(solution)/shard_map/dot_general | solution.py:55
  176.6 70.5 %reduce-scatter.2.cloned.1.call-done = bf16[32,7296]{1,0:T(8,128)(2,1)} async-done(((bf16[512,7296]{1,0:T(8,128)(2,1)}), bf16[32,7296]{1,0:T(8,128)(2,1)}) %reduce-scatter.2.cloned.1.call-update) | async-done | bytes 466960 | tf_op jit(solution)/shard_map/reduce_scatter | solution.py:94
  247.1 2.0 reshape.110
  249.0 9.8 %all-to-all-start.1 = ((bf16[16,2,7296]{2,1,0:T(2,128)(2,1)}), bf16[16,2,7296]{2,1,0:T(2,128)(2,1)S(1)}, u32[]{:S(2)}, u32[]{:S(2)}) async-start(bf16[16,2,7296]{2,1,0:T(2,128)(2,1)} %reshape.110), calls=%async_computation.2 | async-start | bytes 933888 | tf_op jit(solution)/shard_map/all_to_all | solution.py:99
  258.8 6.4 %fusion.2 = bf16[1,7168,128]{2,1,0:T(8,128)(2,1)} fusion(bf16[512,128]{0,1:T(8,128)(2,1)S(1)} %get-tuple-element.7, bf16[512,14464]{1,0:T(8,128)(2,1)} %all-gather.2.cloned.1.call-done), kind=kOutput, calls=%fused_computation.8 | convolution fusion | flops 940441600 | bytes 9306112 | tf_op jit(solution)/shard_map/dot_general | solution.py:55
  265.2 6.5 %fusion.3 = bf16[1,7168,128]{2,1,0:T(8,128)(2,1)} fusion(bf16[512,14464]{1,0:T(8,128)(2,1)} %all-gather.2.cloned.1.call-done, f32[512]{0:T(512)S(1)} %convert_reduce_fusion, f32[512,128]{0,1:T(8,128)S(1)} %fusion.13, f32[512,128]{0,1:T(8,128)S(1)} %get-tuple-element.11), kind=kOutput, calls=%fused_computation.9 | convolution fusion | flops 940900352 | bytes 9701376 | tf_op jit(solution)/shard_map/dot_general | solution.py:55
  271.7 0.0 all-to-all-done.1
  271.7 0.3 slice.35
  272.1 0.9 fusion.4
  273.0 0.1 copy.53
  273.1 0.1 copy.56
  273.2 0.2 multiply_reduce_fusion.1
  273.4 0.6 copy.52
  (8 shorter events, 0.1 us)
Async XLA Ops:
  7.2 124.0 %all-gather.2.cloned.1.call-start = ((), (), s32[]{:S(2)}) async-start(), calls=%async_computation.3 | async-start | bytes 15736832 | tf_op jit(solution)/shard_map/all_gather | solution.py:82
  11.4 38.4 %copy-start.2 = (bf16[1,3,1,56]{3,1,2,0:T(4,128)(2,1)S(1)}, bf16[1,3,1,56]{3,1,2,0:T(4,128)(2,1)}, u32[]{:S(2)}) copy-start(bf16[1,3,1,56]{3,1,2,0:T(4,128)(2,1)} %param.15) | copy-start | bytes 1012
  11.4 120.8 %copy-start.3 = (bf16[1,7168,128]{2,1,0:T(8,128)(2,1)S(1)}, bf16[1,7168,128]{2,1,0:T(8,128)(2,1)}, u32[]{:S(2)}) copy-start(bf16[1,7168,128]{2,1,0:T(8,128)(2,1)} %param.14) | copy-start | bytes 5505028
  49.8 197.3 %reduce-scatter.2.cloned.1.call-start = ((), (), s32[]{:S(2)}) async-start(), calls=%async_computation.4 | async-start | bytes 7938048 | tf_op jit(solution)/shard_map/reduce_scatter | solution.py:94
  132.2 6.8 %copy-start.1 = (bf16[1,7168,128]{2,1,0:T(8,128)(2,1)S(1)}, bf16[1,7168,128]{2,1,0:T(8,128)(2,1)}, u32[]{:S(2)}) copy-start(bf16[1,7168,128]{2,1,0:T(8,128)(2,1)} %param.13) | copy-start | bytes 5505028
  139.0 6.8 %copy-start = (bf16[1,7168,128]{2,1,0:T(8,128)(2,1)S(1)}, bf16[1,7168,128]{2,1,0:T(8,128)(2,1)}, u32[]{:S(2)}) copy-start(bf16[1,7168,128]{2,1,0:T(8,128)(2,1)} %param.12) | copy-start | bytes 5505028
  249.0 22.7 %all-to-all-start.1 = ((bf16[16,2,7296]{2,1,0:T(2,128)(2,1)}), bf16[16,2,7296]{2,1,0:T(2,128)(2,1)S(1)}, u32[]{:S(2)}, u32[]{:S(2)}) async-start(bf16[16,2,7296]{2,1,0:T(2,128)(2,1)} %reshape.110), calls=%async_computation.2 | async-start | bytes 933888 | tf_op jit(solution)/shard_map/all_to_all | solution.py:99
Sparse Core Ops, SparseCore 0:
  49.9 81.2 all-gather.1
  170.3 76.7 reduce-scatter.1

commit v2 on v1

--- a/solution.py
+++ b/solution.py
@@ -75,27 +75,35 @@
     gate_block = jnp.pad(send_gates[:, :, None], ((0, 0), (0, 0), (0, LANE - 1)))
     send = jnp.concatenate([send_rows, gate_block], axis=2)
     recv = lax.all_to_all(send, "eg", split_axis=0, concat_axis=0, tiled=True)
-    recv = recv.reshape(experts * capacity, recv.shape[2])
     wgate = dequantize(gate_codes[0], block_scales[0, 0])
     wup = dequantize(up_codes[0], block_scales[0, 1])
     wdown = dequantize(down_codes[0], block_scales[0, 2])
-    gathered = lax.all_gather(recv, "blk", axis=0, tiled=True)
-    feats = gathered[:, :width]
-    cotan = gathered[:, width : 2 * width]
-    gates = gathered[:, 2 * width].astype(jnp.float32)
-    gate_pre = jnp.dot(feats, wgate, preferred_element_type=jnp.float32)
-    up_pre = jnp.dot(feats, wup, preferred_element_type=jnp.float32)
-    down_back = jnp.dot(cotan, wdown, preferred_element_type=jnp.float32)
-    hidden, grad_gate, grad_up, gated_hidden = backward_math(gate_pre, up_pre, down_back, gates)
-    contrib = project_back(grad_gate, grad_up, wgate, wup).astype(jnp.bfloat16)
-    scores = jnp.sum(hidden * down_back, axis=1).astype(jnp.bfloat16)
-    score_block = jnp.pad(scores[:, None], ((0, 0), (0, LANE - 1)))
-    partial_rows = jnp.concatenate([contrib, score_block], axis=1)
-    summed = lax.psum_scatter(partial_rows, "blk", scatter_dimension=0, tiled=True)
-    gate_grad = row_sum(feats, grad_gate).astype(jnp.bfloat16)[None]
-    up_grad = row_sum(feats, grad_up).astype(jnp.bfloat16)[None]
-    down_grad = row_sum(cotan, gated_hidden).astype(jnp.bfloat16)[None]
-    summed = summed.reshape(experts, capacity, summed.shape[1])
+    summed_slots = []
+    grads = None
+    for slot in range(capacity):
+        gathered = lax.all_gather(recv[:, slot, :], "blk", axis=0, tiled=True)
+        feats = gathered[:, :width]
+        cotan = gathered[:, width : 2 * width]
+        gates = gathered[:, 2 * width].astype(jnp.float32)
+        gate_pre = jnp.dot(feats, wgate, preferred_element_type=jnp.float32)
+        up_pre = jnp.dot(feats, wup, preferred_element_type=jnp.float32)
+        down_back = jnp.dot(cotan, wdown, preferred_element_type=jnp.float32)
+        hidden, grad_gate, grad_up, gated_hidden = backward_math(
+            gate_pre, up_pre, down_back, gates
+        )
+        contrib = project_back(grad_gate, grad_up, wgate, wup).astype(jnp.bfloat16)
+        scores = jnp.sum(hidden * down_back, axis=1).astype(jnp.bfloat16)
+        score_block = jnp.pad(scores[:, None], ((0, 0), (0, LANE - 1)))
+        partial_rows = jnp.concatenate([contrib, score_block], axis=1)
+        summed_slots.append(lax.psum_scatter(partial_rows, "blk", scatter_dimension=0, tiled=True))
+        chunk = (
+            row_sum(feats, grad_gate),
+            row_sum(feats, grad_up),
+            row_sum(cotan, gated_hidden),
+        )
+        grads = chunk if grads is None else tuple(a + b for a, b in zip(grads, chunk))
+    gate_grad, up_grad, down_grad = (g.astype(jnp.bfloat16)[None] for g in grads)
+    summed = jnp.stack(summed_slots, axis=1)
     home = lax.all_to_all(summed, "eg", split_axis=0, concat_axis=0, tiled=True)
     grad_tokens = jnp.einsum(
         "tec,ecd->td", placed_low, home[:, :, :width], preferred_element_type=jnp.float32

time: 282 us -> 330 us (1.17)
  waiting for transfers between devices: 152 us -> 181 us
  matrix products: 52.7 us -> 68.7 us
    reduce_scatter x1 -> x2, waiting for transfers between devices: 70.5 us -> 103 us  [on_device(): lax.psum_scatter(partial_rows, 'blk', scatter_dimension=0, tiled=True)]
    all_gather x1 -> x2, waiting for transfers between devices: 81.2 us -> 71.6 us  [on_device(): gathered = lax.all_gather(recv[:, slot, :], 'blk', axis=0, tiled=True)]
    all_to_all x1, waiting for transfers between devices: 0.01 us -> 6.32 us  [on_device(): home = lax.all_to_all(summed, 'eg', split_axis=0, concat_axis=0, tiled=True)]
    dot_general x1 -> x2, matrix products: 6.82 us -> 12.2 us  [on_device(): gate_pre = jnp.dot(feats, wgate, preferred_element_type=jnp.float32)]
    dot_general x1 -> x2, matrix products: 6.78 us -> 11 us  [on_device(): up_pre = jnp.dot(feats, wup, preferred_element_type=jnp.float32)]
    dot_general x1 -> x2, matrix products: 4.79 us -> 8.7 us  [project_back(): lax.dot_general(grad_gate, wgate, contract_cols, preferred_element_type=j...]
    dot_general x1 -> x2, matrix products: 6.78 us -> 9.95 us  [on_device(): down_back = jnp.dot(cotan, wdown, preferred_element_type=jnp.float32)]
    dot_general x3 -> x6, matrix products: 19.4 us -> 17.4 us  [row_sum(): lax.dot_general(left, right, (((0,), (0,)), ((), ())), preferred_element_...]
  transfers between devices with their start and end apart: 3 -> 5, of which waited for: 2 -> 5; matrix products, arithmetic and copies ran while one was open for 7% -> 22% of each run, Pallas kernels for 0% -> 0%
where the time goes in v2:
time: 330 us; the launch traced here: 329 us
  waiting for transfers between devices  181 us (55%)
  matrix products  68.7 us (21%)
  blocking collectives  36.3 us (11%)
  between operations  14.1 us (4%)
  starting transfers between devices  10.1 us (3%)
  other arithmetic  10.1 us (3%)
  local copies, waits for them, and re-layouts  8.43 us (3%)
    reduce_scatter x2, waiting for transfers between devices, on_device(): lax.psum_scatter(partial_rows, 'blk', scatter_dimension=0, tiled=True)  103 us
    all_gather x2, waiting for transfers between devices, on_device(): gathered = lax.all_gather(recv[:, slot, :], 'blk', axis=0, tiled=True)  71.6 us
    all_to_all x1, blocking collectives, on_device(): recv = lax.all_to_all(send, 'eg', split_axis=0, concat_axis=0, tiled=True)  36.3 us
    dot_general x6, matrix products, row_sum(): lax.dot_general(left, right, (((0,), (0,)), ((), ())), preferred_element_...  17.4 us
    dot_general x2, matrix products, on_device(): gate_pre = jnp.dot(feats, wgate, preferred_element_type=jnp.float32)  12.2 us
    dot_general x2, matrix products, on_device(): up_pre = jnp.dot(feats, wup, preferred_element_type=jnp.float32)  11 us
    dot_general x2, matrix products, on_device(): down_back = jnp.dot(cotan, wdown, preferred_element_type=jnp.float32)  9.95 us
    all_to_all x1, starting transfers between devices, on_device(): home = lax.all_to_all(summed, 'eg', split_axis=0, concat_axis=0, tiled=True)  9.8 us
  transfers between devices with their start and end apart: 5, of which 5 were waited for; matrix products, arithmetic and copies ran while one was open for 22% of the time, Pallas kernels for 0%

profile of v2, /device:TPU:32, one launch (start us, length us, event | category | flops | bytes accessed | tf_op | source)
XLA Modules:
  0.0 328.6 jit_solution(6293411121901217036)
XLA Ops:
  7.2 0.8 fusion.54
  8.0 0.7 fusion.47
  8.8 0.1 copy.42
  8.9 0.7 bitcast_convert_fusion.4
  9.6 0.1 multiply_reduce_fusion.1
  9.8 0.1 copy.43
  10.0 1.4 convolution_convert_fusion
  11.4 0.7 copy.44
  12.1 36.3 %all_to_all.10 = bf16[16,2,14464]{2,1,0:T(2,128)(2,1)S(1)} all-to-all(bf16[16,2,14464]{2,1,0:T(2,128)(2,1)S(1)} %copy.44), channel_id=1, replica_groups=mesh['eg'=16,'blk'=16] {'eg'}, dimensions={0} | all-to-all | bytes 1851392 | tf_op jit(solution)/shard_map/all_to_all | solution.py:77
  48.5 1.3 fusion.68
  49.8 0.8 copy.69
  50.6 0.8 copy.70
  51.5 0.2 reduce-scatter.3.cloned.1.call-start
  51.9 45.3 %all-gather.5.cloned.1.call-done = bf16[256,1,14464]{2,0,1:T(8,128)(2,1)} async-done(((bf16[16,1,14464]{2,0,1:T(8,128)(2,1)}), bf16[256,1,14464]{2,0,1:T(8,128)(2,1)}) %all-gather.5.cloned.1.call-update) | async-done | bytes 7405584 | tf_op jit(solution)/shard_map/all_gather | solution.py:84
  97.2 0.9 convert_reduce_fusion.1
  98.1 5.0 %fusion.21 = f32[256,128]{0,1:T(8,128)S(1)} fusion(bf16[256,14464]{1,0:T(8,128)(2,1)} %bitcast.87, bf16[1,7168,128]{2,1,0:T(8,128)(2,1)} %param.14, f32[7168]{0:T(1024)S(1)} %get-tuple-element.19), kind=kOutput, calls=%fused_computation.32 | convolution fusion | flops 472514560 | bytes 5664768 | tf_op jit(solution)/shard_map/dot_general | solution.py:90
  103.1 5.1 %fusion.35 = f32[256,128]{0,1:T(8,128)S(1)} fusion(bf16[256,14464]{1,0:T(8,128)(2,1)} %bitcast.88, bf16[1,7168,128]{2,1,0:T(8,128)(2,1)} %param.13, f32[7168]{0:T(1024)S(1)} %broadcast_bitcast_fusion.1), kind=kOutput, calls=%fused_computation.46 | convolution fusion | flops 472514560 | bytes 5664768 | tf_op jit(solution)/shard_map/dot_general | solution.py:89
  108.2 5.8 %multiply_convert_fusion.5 = (bf16[256,128]{0,1:T(8,128)(2,1)S(1)}, bf16[256]{0:T(256)(128)(2,1)S(1)}, bf16[256,128]{0,1:T(8,128)(2,1)S(1)}, f32[256,128]{0,1:T(8,128)S(1)}) fusion(f32[256,128]{0,1:T(8,128)S(1)} %fusion.35, f32[256,128]{0,1:T(8,128)S(1)} %fusion.21, f32[256]{0:T(256)S(1)} %convert_reduce_fusion.1, bf16[1,7168,128]{2,1,0:T(8,128)(2,1)S(1)} %copy-done, ...), kind=kOutput, calls=%fused_computation.70 | convolution fusion | flops 473104128 | bytes 6059520 | tf_op jit(solution)/shard_map/dot_general | solution.py:88
  114.0 0.1 convert_element_type.222
  114.1 4.3 %fusion.65 = f32[256,7168]{1,0:T(8,128)S(1)} fusion(bf16[256,128]{0,1:T(8,128)(2,1)S(1)} %get-tuple-element.7, bf16[1,7168,128]{2,1,0:T(8,128)(2,1)S(1)} %copy-done, f32[7168]{0:T(1024)S(1)} %get-tuple-element.18), kind=kOutput, calls=%fused_computation.98 | convolution fusion | flops 472514560 | bytes 9269248 | tf_op jit(solution)/shard_map/dot_general | solution.py:46
  118.5 3.6 %fusion = bf16[256,7168]{1,0:T(8,128)(2,1)S(1)} fusion(f32[256,7168]{1,0:T(8,128)S(1)} %fusion.65, bf16[256,128]{0,1:T(8,128)(2,1)S(1)} %get-tuple-element.11, bf16[1,7168,128]{2,1,0:T(8,128)(2,1)S(1)} %copy-done.1, f32[7168]{0:T(1024)S(1)} %broadcast_bitcast_fusion.1), kind=kOutput, calls=%fused_computation.3 | convolution fusion | flops 476184576 | bytes 12939264 | tf_op jit(solution)/shard_map/dot_general | solution.py:49
  122.1 2.1 fusion.11
  124.3 26.3 %all-gather.7.cloned.1.call-done = bf16[256,1,14464]{2,0,1:T(8,128)(2,1)} async-done(((bf16[16,1,14464]{2,0,1:T(8,128)(2,1)}), bf16[256,1,14464]{2,0,1:T(8,128)(2,1)}) %all-gather.7.cloned.1.call-update) | async-done | bytes 7405584 | tf_op jit(solution)/shard_map/all_gather | solution.py:84
  150.6 1.1 convert_reduce_fusion
  151.7 5.0 %fusion.17 = f32[256,128]{0,1:T(8,128)S(1)} fusion(bf16[256,14464]{1,0:T(8,128)(2,1)} %bitcast.76, bf16[1,7168,128]{2,1,0:T(8,128)(2,1)} %param.14, f32[7168]{0:T(1024)S(1)} %get-tuple-element.19), kind=kOutput, calls=%fused_computation.28 | convolution fusion | flops 472514560 | bytes 5664768 | tf_op jit(solution)/shard_map/dot_general | solution.py:90
  156.7 5.9 %fusion.27 = f32[256,128]{0,1:T(8,128)S(1)} fusion(bf16[256,14464]{1,0:T(8,128)(2,1)} %bitcast.77, bf16[1,7168,128]{2,1,0:T(8,128)(2,1)S(1)} %copy-done.2, f32[7168]{0:T(1024)S(1)} %broadcast_bitcast_fusion.1), kind=kOutput, calls=%fused_computation.38 | convolution fusion | flops 472514560 | bytes 5664768 | tf_op jit(solution)/shard_map/dot_general | solution.py:89
  162.6 6.4 %multiply_convert_fusion.3 = (bf16[256,128]{0,1:T(8,128)(2,1)S(1)}, bf16[256]{0:T(256)(128)(2,1)S(1)}, bf16[256,128]{0,1:T(8,128)(2,1)S(1)}, f32[256,128]{0,1:T(8,128)}) fusion(f32[256,128]{0,1:T(8,128)S(1)} %fusion.27, f32[256,128]{0,1:T(8,128)S(1)} %fusion.17, f32[256]{0:T(256)S(1)} %convert_reduce_fusion, bf16[1,7168,128]{2,1,0:T(8,128)(2,1)S(1)} %copy-done, ...), kind=kOutput, calls=%fused_computation.65 | convolution fusion | flops 473104128 | bytes 6059520 | tf_op jit(solution)/shard_map/dot_general | solution.py:88
  169.1 4.3 %fusion.62 = f32[256,7168]{1,0:T(8,128)S(1)} fusion(bf16[256,128]{0,1:T(8,128)(2,1)S(1)} %get-tuple-element.9, bf16[1,7168,128]{2,1,0:T(8,128)(2,1)S(1)} %copy-done, f32[7168]{0:T(1024)S(1)} %get-tuple-element.18), kind=kOutput, calls=%fused_computation.97 | convolution fusion | flops 472514560 | bytes 9269248 | tf_op jit(solution)/shard_map/dot_general | solution.py:46
  173.5 3.6 %fusion.1 = bf16[256,7168]{1,0:T(8,128)(2,1)S(1)} fusion(f32[256,7168]{1,0:T(8,128)S(1)} %fusion.62, bf16[256,128]{0,1:T(8,128)(2,1)S(1)} %get-tuple-element.12, bf16[1,7168,128]{2,1,0:T(8,128)(2,1)S(1)} %copy-done.2, f32[7168]{0:T(1024)S(1)} %broadcast_bitcast_fusion.1), kind=kOutput, calls=%fused_computation.4 | convolution fusion | flops 476184576 | bytes 12939264 | tf_op jit(solution)/shard_map/dot_general | solution.py:49
  177.1 2.1 fusion.12
  179.3 3.4 %fusion.29 = f32[7168,128]{1,0:T(8,128)S(1)} fusion(bf16[256,128]{0,1:T(8,128)(2,1)S(1)} %get-tuple-element.11, bf16[256,14464]{1,0:T(8,128)(2,1)} %bitcast.90), kind=kOutput, calls=%fused_computation.40 | convolution fusion | flops 469762048 | bytes 7405568 | tf_op jit(solution)/shard_map/dot_general | solution.py:55
  182.7 3.4 %fusion.31 = f32[7168,128]{1,0:T(8,128)S(1)} fusion(bf16[256,128]{0,1:T(8,128)(2,1)S(1)} %get-tuple-element.7, bf16[256,14464]{1,0:T(8,128)(2,1)} %bitcast.91), kind=kOutput, calls=%fused_computation.42 | convolution fusion | flops 469762048 | bytes 7405568 | tf_op jit(solution)/shard_map/dot_general | solution.py:55
  186.1 2.4 fusion.6
  188.5 2.4 fusion.7
  190.9 32.5 %reduce-scatter.3.cloned.1.call-done = bf16[16,7296]{1,0:T(8,128)(2,1)} async-done(((bf16[256,7296]{1,0:T(8,128)(2,1)}), bf16[16,7296]{1,0:T(8,128)(2,1)}) %reduce-scatter.3.cloned.1.call-update) | async-done | bytes 233488 | tf_op jit(solution)/shard_map/reduce_scatter | solution.py:98
  223.4 70.3 %reduce-scatter.5.cloned.1.call-done = bf16[16,7296]{1,0:T(8,128)(2,1)} async-done(((bf16[256,7296]{1,0:T(8,128)(2,1)}), bf16[16,7296]{1,0:T(8,128)(2,1)}) %reduce-scatter.5.cloned.1.call-update) | async-done | bytes 233488 | tf_op jit(solution)/shard_map/reduce_scatter | solution.py:98
  293.7 1.3 pad_maximum_fusion
  295.0 1.1 copy.49
  296.1 9.8 %all-to-all-start.1 = ((bf16[16,2,7296]{2,1,0:T(2,128)(2,1)}), bf16[16,2,7296]{2,1,0:T(2,128)(2,1)}, u32[]{:S(2)}, u32[]{:S(2)}) async-start(bf16[16,2,7296]{2,1,0:T(2,128)(2,1)} %copy.49), calls=%async_computation.3 | async-start | bytes 933888 | tf_op jit(solution)/shard_map/all_to_all | solution.py:107
  306.0 3.4 %fusion.19 = f32[7168,128]{1,0:T(8,128)S(1)} fusion(bf16[256,14464]{1,0:T(8,128)(2,1)} %bitcast.92, f32[256]{0:T(256)} %copy-done.6, f32[256,128]{0,1:T(8,128)S(1)} %fusion.35, f32[256,128]{0,1:T(8,128)S(1)} %get-tuple-element.17), kind=kOutput, calls=%fused_computation.30 | convolution fusion | flops 469991424 | bytes 7603200 | tf_op jit(solution)/shard_map/dot_general | solution.py:55
  309.4 2.4 fusion.5
  311.8 6.3 %all-to-all-done.1 = bf16[16,2,7296]{2,1,0:T(2,128)(2,1)} async-done(((bf16[16,2,7296]{2,1,0:T(2,128)(2,1)}), bf16[16,2,7296]{2,1,0:T(2,128)(2,1)}, u32[]{:S(2)}, u32[]{:S(2)}) %all-to-all-start.1) | async-done | bytes 466976 | tf_op jit(solution)/shard_map/all_to_all | solution.py:107
  318.1 1.3 slice.60
  319.4 0.9 fusion.8
  320.3 0.7 slice.61
  321.0 0.1 copy.68
  321.2 0.2 multiply_reduce_fusion
  321.4 0.6 copy.67
  (50 shorter events, 0.9 us)
Async XLA Ops:
  7.2 90.0 %all-gather.5.cloned.1.call-start = ((), (), s32[]{:S(2)}) async-start(), calls=%async_computation.6 | async-start | bytes 7868416 | tf_op jit(solution)/shard_map/all_gather | solution.py:84
  48.5 3.3 copy-start.9
  50.6 100.0 %all-gather.7.cloned.1.call-start = ((), (), s32[]{:S(2)}) async-start(), calls=%async_computation.7 | async-start | bytes 7868416 | tf_op jit(solution)/shard_map/all_gather | solution.py:84
  51.5 171.9 %reduce-scatter.3.cloned.1.call-start = ((), (), s32[]{:S(2)}) async-start(), calls=%async_computation.4 | async-start | bytes 3969024 | tf_op jit(solution)/shard_map/reduce_scatter | solution.py:98
  98.1 10.1 %copy-start.6 = (f32[256]{0:T(256)}, f32[256]{0:T(256)S(1)}, u32[]{:S(2)}) copy-start(f32[256]{0:T(256)S(1)} %convert_reduce_fusion.1) | copy-start | bytes 3076
  103.1 5.1 %copy-start = (bf16[1,7168,128]{2,1,0:T(8,128)(2,1)S(1)}, bf16[1,7168,128]{2,1,0:T(8,128)(2,1)}, u32[]{:S(2)}) copy-start(bf16[1,7168,128]{2,1,0:T(8,128)(2,1)} %param.12) | copy-start | bytes 5505028
  114.1 4.4 %copy-start.1 = (bf16[1,7168,128]{2,1,0:T(8,128)(2,1)S(1)}, bf16[1,7168,128]{2,1,0:T(8,128)(2,1)}, u32[]{:S(2)}) copy-start(bf16[1,7168,128]{2,1,0:T(8,128)(2,1)} %param.13) | copy-start | bytes 5505028
  124.2 169.5 %reduce-scatter.5.cloned.1.call-start = ((), (), s32[]{:S(2)}) async-start(), calls=%async_computation.5 | async-start | bytes 3969024 | tf_op jit(solution)/shard_map/reduce_scatter | solution.py:98
  150.6 6.1 %copy-start.2 = (bf16[1,7168,128]{2,1,0:T(8,128)(2,1)S(1)}, bf16[1,7168,128]{2,1,0:T(8,128)(2,1)}, u32[]{:S(2)}) copy-start(bf16[1,7168,128]{2,1,0:T(8,128)(2,1)} %param.13) | copy-start | bytes 5505028
  151.7 10.9 %copy-start.7 = (f32[256]{0:T(256)}, f32[256]{0:T(256)S(1)}, u32[]{:S(2)}) copy-start(f32[256]{0:T(256)S(1)} %convert_reduce_fusion) | copy-start | bytes 3076
  162.6 6.5 %copy-start.3 = (f32[256,128]{0,1:T(8,128)}, f32[256,128]{0,1:T(8,128)S(1)}, u32[]{:S(2)}) copy-start(f32[256,128]{0,1:T(8,128)S(1)} %fusion.27) | copy-start | bytes 393220
  179.3 6.8 %slice-start = ((s8[7405568]{0:T(1024)(128)(4,1)}), s8[4194304]{0:T(1024)(128)(4,1)S(1)}, s32[]{:S(2)}) async-start(s8[7405568]{0:T(1024)(128)(4,1)} %bitcast.79), calls=%async_computation.8 | async-start | bytes 8388608
  182.7 3.4 %slice-start.1 = ((s8[7405568]{0:T(1024)(128)(4,1)}), s8[3211264]{0:T(1024)(128)(4,1)S(1)}, s32[]{:S(2)}) async-start(s8[7405568]{0:T(1024)(128)(4,1)} %bitcast.79), calls=%async_computation.9 | async-start | bytes 6422528
  293.7 15.6 %slice-start.2 = ((s8[7405568]{0:T(1024)(128)(4,1)}), s8[3211264]{0:T(1024)(128)(4,1)S(1)}, s32[]{:S(2)}) async-start(s8[7405568]{0:T(1024)(128)(4,1)} %bitcast.83), calls=%async_computation.10 | async-start | bytes 6422528
  296.1 22.0 %all-to-all-start.1 = ((bf16[16,2,7296]{2,1,0:T(2,128)(2,1)}), bf16[16,2,7296]{2,1,0:T(2,128)(2,1)}, u32[]{:S(2)}, u32[]{:S(2)}) async-start(bf16[16,2,7296]{2,1,0:T(2,128)(2,1)} %copy.49), calls=%async_computation.3 | async-start | bytes 933888 | tf_op jit(solution)/shard_map/all_to_all | solution.py:107
  305.9 3.4 %slice-start.3 = ((s8[7405568]{0:T(1024)(128)(4,1)}), s8[4194304]{0:T(1024)(128)(4,1)S(1)}, s32[]{:S(2)}) async-start(s8[7405568]{0:T(1024)(128)(4,1)} %bitcast.83), calls=%async_computation.11 | async-start | bytes 8388608
  305.9 3.4 %copy-start.4 = (f32[256,128]{0,1:T(8,128)S(1)}, f32[256,128]{0,1:T(8,128)}, u32[]{:S(2)}) copy-start(f32[256,128]{0,1:T(8,128)} %copy-done.3) | copy-start | bytes 393220
  305.9 3.4 %copy-start.5 = (f32[256,128]{0,1:T(8,128)S(1)}, f32[256,128]{0,1:T(8,128)}, u32[]{:S(2)}) copy-start(f32[256,128]{0,1:T(8,128)} %get-tuple-element.16) | copy-start | bytes 393220
  305.9 3.4 %copy-start.8 = (f32[256]{0:T(256)S(1)}, f32[256]{0:T(256)}, u32[]{:S(2)}) copy-start(f32[256]{0:T(256)} %copy-done.7) | copy-start | bytes 3076
Sparse Core Ops, SparseCore 0:
  50.7 46.3 all-gather.4
  99.6 50.9 all-gather.6
  153.1 70.1 reduce-scatter.2
  225.8 67.8 reduce-scatter.4

commit v3 on v1

--- a/solution.py
+++ b/solution.py
@@ -79,22 +79,33 @@
     wgate = dequantize(gate_codes[0], block_scales[0, 0])
     wup = dequantize(up_codes[0], block_scales[0, 1])
     wdown = dequantize(down_codes[0], block_scales[0, 2])
+    hid = wgate.shape[1]
+    wboth = jnp.concatenate([wgate, wup], axis=1)
+    wboth_ext = jnp.pad(wboth, ((0, LANE), (0, 0)))
     gathered = lax.all_gather(recv, "blk", axis=0, tiled=True)
     feats = gathered[:, :width]
     cotan = gathered[:, width : 2 * width]
     gates = gathered[:, 2 * width].astype(jnp.float32)
-    gate_pre = jnp.dot(feats, wgate, preferred_element_type=jnp.float32)
-    up_pre = jnp.dot(feats, wup, preferred_element_type=jnp.float32)
+    both_pre = jnp.dot(feats, wboth, preferred_element_type=jnp.float32)
+    gate_pre = both_pre[:, :hid]
+    up_pre = both_pre[:, hid:]
     down_back = jnp.dot(cotan, wdown, preferred_element_type=jnp.float32)
     hidden, grad_gate, grad_up, gated_hidden = backward_math(gate_pre, up_pre, down_back, gates)
-    contrib = project_back(grad_gate, grad_up, wgate, wup).astype(jnp.bfloat16)
-    scores = jnp.sum(hidden * down_back, axis=1).astype(jnp.bfloat16)
-    score_block = jnp.pad(scores[:, None], ((0, 0), (0, LANE - 1)))
-    partial_rows = jnp.concatenate([contrib, score_block], axis=1)
+    grad_both = jnp.concatenate([grad_gate, grad_up], axis=1)
+    back = lax.dot_general(
+        grad_both, wboth_ext, (((1,), (1,)), ((), ())), preferred_element_type=jnp.float32
+    )
+    scores = jnp.sum(hidden * down_back, axis=1).astype(jnp.bfloat16).astype(jnp.float32)
+    column = lax.broadcasted_iota(jnp.int32, back.shape, 1)
+    partial_rows = jnp.where(column == width, scores[:, None], back).astype(jnp.bfloat16)
     summed = lax.psum_scatter(partial_rows, "blk", scatter_dimension=0, tiled=True)
-    gate_grad = row_sum(feats, grad_gate).astype(jnp.bfloat16)[None]
-    up_grad = row_sum(feats, grad_up).astype(jnp.bfloat16)[None]
+    both_grad = row_sum(feats, grad_both).astype(jnp.bfloat16)
+    gate_grad = both_grad[None, :, :hid]
+    up_grad = both_grad[None, :, hid:]
     down_grad = row_sum(cotan, gated_hidden).astype(jnp.bfloat16)[None]
+    summed, gate_grad, up_grad, down_grad = lax.optimization_barrier(
+        (summed, gate_grad, up_grad, down_grad)
+    )
     summed = summed.reshape(experts, capacity, summed.shape[1])
     home = lax.all_to_all(summed, "eg", split_axis=0, concat_axis=0, tiled=True)
     grad_tokens = jnp.einsum(

time: 282 us -> 261 us (0.926)
  blocking collectives: 36.3 us -> 57.9 us
  matrix products: 52.7 us -> 33.2 us
  waiting for transfers between devices: 152 us -> 133 us
  starting transfers between devices: 9.84 us -> 0.08 us
  other arithmetic: 10.2 us -> 14.1 us
    all_to_all x0 -> x1, blocking collectives: none -> 21.6 us  [on_device(): home = lax.all_to_all(summed, 'eg', split_axis=0, concat_axis=0, tiled=True)]
    dot_general x4 -> x2, matrix products: 24.3 us -> 12 us  [the longest x1 6.16 us: on_device(): lax.dot_general(grad_both, wboth_ext, (((1,), (1,)), ((), ())), preferred...]
    all_gather x1, waiting for transfers between devices: 81.2 us -> 69.4 us  [on_device(): gathered = lax.all_gather(recv, 'blk', axis=0, tiled=True)]
    all_to_all x1 -> x0, starting transfers between devices: 9.76 us -> none  [on_device(): home = lax.all_to_all(summed, 'eg', split_axis=0, concat_axis=0, tiled=True)]
    convert_element_type x0 -> x2, other arithmetic: none -> 8.32 us  [dequantize(): return scaled.reshape(rows_in, cols_in).astype(jnp.bfloat16)]
    dot_general x3 -> x2, matrix products: 19.4 us -> 11.7 us  [row_sum(): lax.dot_general(left, right, (((0,), (0,)), ((), ())), preferred_element_...]
    reduce_scatter x1, waiting for transfers between devices: 70.5 us -> 63.1 us  [on_device(): lax.psum_scatter(partial_rows, 'blk', scatter_dimension=0, tiled=True)]
    concatenate x1, other arithmetic: 6.57 us -> 2.19 us  [on_device(): wboth = jnp.concatenate([wgate, wup], axis=1)]
  transfers between devices with their start and end apart: 3 -> 2, of which waited for: 2 -> 2; matrix products, arithmetic and copies ran while one was open for 7% -> 9% of each run, Pallas kernels for 0% -> 0%
where the time goes in v3:
time: 261 us; the launch traced here: 260 us
  waiting for transfers between devices  133 us (51%)
  blocking collectives  57.9 us (22%)
  matrix products  33.2 us (13%)
  between operations  14.2 us (5%)
  other arithmetic  14.1 us (5%)
  local copies, waits for them, and re-layouts  8.17 us (3%)
    all_gather x1, waiting for transfers between devices, on_device(): gathered = lax.all_gather(recv, 'blk', axis=0, tiled=True)  69.4 us
    reduce_scatter x1, waiting for transfers between devices, on_device(): lax.psum_scatter(partial_rows, 'blk', scatter_dimension=0, tiled=True)  63.1 us
    all_to_all x1, blocking collectives, on_device(): recv = lax.all_to_all(send, 'eg', split_axis=0, concat_axis=0, tiled=True)  36.3 us
    all_to_all x1, blocking collectives, on_device(): home = lax.all_to_all(summed, 'eg', split_axis=0, concat_axis=0, tiled=True)  21.6 us
    dot_general x2, matrix products, row_sum(): lax.dot_general(left, right, (((0,), (0,)), ((), ())), preferred_element_...  11.7 us
    convert_element_type x2, other arithmetic, dequantize(): return scaled.reshape(rows_in, cols_in).astype(jnp.bfloat16)  8.32 us
    dot_general x1, matrix products, on_device(): down_back = jnp.dot(cotan, wdown, preferred_element_type=jnp.float32)  7.16 us
    dot_general x1, matrix products, on_device(): lax.dot_general(grad_both, wboth_ext, (((1,), (1,)), ((), ())), preferred...  6.16 us
  transfers between devices with their start and end apart: 2, of which 2 were waited for; matrix products, arithmetic and copies ran while one was open for 9% of the time, Pallas kernels for 0%

profile of v3, /device:TPU:32, one launch (start us, length us, event | category | flops | bytes accessed | tf_op | source)
XLA Modules:
  0.0 260.3 jit_solution(12313640950780743697)
XLA Ops:
  7.2 0.0 all-gather.2.cloned.1.call-start
  7.2 0.8 fusion.29
  8.0 0.7 fusion.22
  8.7 0.7 bitcast_convert_fusion.4
  9.4 0.1 copy.52
  9.5 0.1 copy.29
  9.6 0.1 multiply_reduce_fusion.2
  9.8 0.1 copy.56
  9.8 0.1 copy.30
  10.0 1.4 convolution_convert_fusion
  11.4 0.1 fusion.16
  11.4 0.0 copy-start.2
  11.4 0.7 copy.31
  12.2 36.3 %all_to_all.10 = bf16[16,2,14464]{2,1,0:T(2,128)(2,1)S(1)} all-to-all(bf16[16,2,14464]{2,1,0:T(2,128)(2,1)S(1)} %copy.31), channel_id=1, replica_groups=mesh['eg'=16,'blk'=16] {'eg'}, dimensions={0} | all-to-all | bytes 1851392 | tf_op jit(solution)/shard_map/all_to_all | solution.py:77
  48.5 1.3 reshape.105
  49.7 0.0 all-gather.2.cloned.1.call-update
  49.8 0.0 reduce-scatter.2.cloned.1.call-start
  49.8 0.0 copy-done.2
  49.9 0.1 broadcast_bitcast_fusion.2
  49.9 0.1 broadcast_bitcast_fusion
  50.0 4.2 %fusion.11 = bf16[7168,128]{1,0:T(8,128)(2,1)S(1)} fusion(bf16[1,7168,128]{2,1,0:T(8,128)(2,1)} %param.12, f32[7168]{0:T(1024)S(1)} %broadcast_bitcast_fusion.2), kind=kLoop, calls=%fused_computation.20 | loop fusion | flops 2752512 | bytes 3698688 | tf_op jit(solution)/shard_map/convert_element_type | solution.py:15
  54.2 4.2 %fusion.10 = bf16[7168,128]{1,0:T(8,128)(2,1)S(1)} fusion(bf16[1,7168,128]{2,1,0:T(8,128)(2,1)} %param.13, f32[7168]{0:T(1024)S(1)} %get-tuple-element.22), kind=kLoop, calls=%fused_computation.18 | loop fusion | flops 2752512 | bytes 3698688 | tf_op jit(solution)/shard_map/convert_element_type | solution.py:15
  58.3 0.0 copy-start
  58.4 1.2 copy-done
  59.6 2.2 pad_maximum_fusion
  61.8 69.4 %all-gather.2.cloned.1.call-done = bf16[512,14464]{1,0:T(8,128)(2,1)} async-done(((bf16[32,14464]{1,0:T(8,128)(2,1)}), bf16[512,14464]{1,0:T(8,128)(2,1)}) %all-gather.2.cloned.1.call-update) | async-done | bytes 14811152 | tf_op jit(solution)/shard_map/all_gather | solution.py:85
  131.2 1.0 convert_reduce_fusion
  132.2 0.0 copy-start.3
  132.2 5.8 %fusion.6 = f32[512,256]{0,1:T(8,128)S(1)} fusion(bf16[512,14464]{1,0:T(8,128)(2,1)} %all-gather.2.cloned.1.call-done, bf16[7168,128]{1,0:T(8,128)(2,1)} %copy-done, bf16[7168,128]{1,0:T(8,128)(2,1)S(1)} %fusion.11), kind=kOutput, calls=%fused_computation.11 | convolution fusion | flops 1886388224 | bytes 11534336 | tf_op jit(solution)/shard_map/dot_general | solution.py:89
  138.1 0.0 copy-done.3
  138.1 0.0 copy-start.1
  138.1 7.2 %multiply_convert_fusion.2 = (bf16[512,128]{0,1:T(8,128)(2,1)S(1)}, bf16[512,128]{0,1:T(8,128)(2,1)S(1)}, bf16[512]{0:T(512)(128)(2,1)S(1)}) fusion(f32[512,256]{0,1:T(8,128)S(1)} %fusion.6, f32[512]{0:T(512)S(1)} %convert_reduce_fusion, bf16[1,7168,128]{2,1,0:T(8,128)(2,1)S(1)} %copy-done.3, f32[7168]{0:T(1024)S(1)} %get-tuple-element.21, ...), kind=kOutput, calls=%fused_computation.33 | convolution fusion | flops 943455744 | bytes 9993216 | tf_op jit(solution)/shard_map/dot_general | solution.py:92
  145.3 0.0 copy-done.1
  145.3 6.2 %select_convert_fusion = bf16[512,7296]{1,0:T(8,128)(2,1)} fusion(bf16[512]{0:T(512)(128)(2,1)S(1)} %get-tuple-element.17, pred[7296]{0:T(1024)(128)(4,1)S(1)} %iota_compare_fusion.1, bf16[7168,256]{1,0:T(8,128)(2,1)S(1)} %copy-done.1, bf16[512,128]{0,1:T(8,128)(2,1)S(1)} %get-tuple-element.16, bf16[512,128]{0,1:T(8,128)(2,1)S(1)} %get-tuple-element.15), kind=kOutput, calls=%fused_computation.1 | convolution fusion | flops 1916862464 | bytes 11411584 | tf_op jit(solution)/shard_map/dot_general | solution.py:95
  151.4 0.0 reduce-scatter.2.cloned.1.call-update
  151.5 6.5 %fusion = bf16[1,7168,128]{2,1,0:T(8,128)(2,1)} fusion(bf16[512,14464]{1,0:T(8,128)(2,1)} %all-gather.2.cloned.1.call-done, f32[512]{0:T(512)S(1)} %convert_reduce_fusion, f32[512,256]{0,1:T(8,128)S(1)} %fusion.6), kind=kOutput, calls=%fused_computation.4 | convolution fusion | flops 940900352 | bytes 9701376 | tf_op jit(solution)/shard_map/dot_general | solution.py:55
  158.0 5.2 %convolution_convert_fusion.1 = bf16[7168,256]{1,0:T(8,128)(2,1)S(1)} fusion(bf16[512,14464]{1,0:T(8,128)(2,1)} %all-gather.2.cloned.1.call-done, bf16[512,128]{0,1:T(8,128)(2,1)S(1)} %get-tuple-element.16, bf16[512,128]{0,1:T(8,128)(2,1)S(1)} %get-tuple-element.15), kind=kOutput, calls=%fused_computation.2 | convolution fusion | flops 1881407488 | bytes 11272192 | tf_op jit(solution)/shard_map/dot_general | solution.py:55
  163.2 2.1 slice_bitcast_fusion
  165.3 63.1 %reduce-scatter.2.cloned.1.call-done = bf16[32,7296]{1,0:T(8,128)(2,1)} async-done(((bf16[512,7296]{1,0:T(8,128)(2,1)}), bf16[32,7296]{1,0:T(8,128)(2,1)}) %reduce-scatter.2.cloned.1.call-update) | async-done | bytes 466960 | tf_op jit(solution)/shard_map/reduce_scatter | solution.py:101
  228.4 1.2 reshape.106
  229.6 21.6 %all_to_all.11 = bf16[16,2,7296]{2,1,0:T(2,128)(2,1)S(1)} all-to-all(bf16[16,2,7296]{2,1,0:T(2,128)(2,1)S(1)} %reshape.106), channel_id=1, replica_groups=mesh['eg'=16,'blk'=16] {'eg'}, dimensions={0} | all-to-all | bytes 933888 | tf_op jit(solution)/shard_map/all_to_all | solution.py:110
  251.2 0.3 slice.55
  251.5 0.9 fusion.1
  252.4 0.1 copy.50
  252.6 0.1 copy.53
  252.6 0.2 multiply_reduce_fusion.1
  252.8 0.6 copy.49
  (8 shorter events, 0.1 us)
Async XLA Ops:
  7.2 124.0 %all-gather.2.cloned.1.call-start = ((), (), s32[]{:S(2)}) async-start(), calls=%async_computation.3 | async-start | bytes 15736832 | tf_op jit(solution)/shard_map/all_gather | solution.py:85
  11.4 38.4 %copy-start.2 = (bf16[1,3,1,56]{3,1,2,0:T(4,128)(2,1)S(1)}, bf16[1,3,1,56]{3,1,2,0:T(4,128)(2,1)}, u32[]{:S(2)}) copy-start(bf16[1,3,1,56]{3,1,2,0:T(4,128)(2,1)} %param.15) | copy-start | bytes 1012
  49.8 178.6 %reduce-scatter.2.cloned.1.call-start = ((), (), s32[]{:S(2)}) async-start(), calls=%async_computation.4 | async-start | bytes 7938048 | tf_op jit(solution)/shard_map/reduce_scatter | solution.py:101
  58.3 1.2 copy-start
  132.2 5.9 %copy-start.3 = (bf16[1,7168,128]{2,1,0:T(8,128)(2,1)S(1)}, bf16[1,7168,128]{2,1,0:T(8,128)(2,1)}, u32[]{:S(2)}) copy-start(bf16[1,7168,128]{2,1,0:T(8,128)(2,1)} %param.14) | copy-start | bytes 5505028
  138.1 7.2 %copy-start.1 = (bf16[7168,256]{1,0:T(8,128)(2,1)S(1)}, bf16[7168,256]{1,0:T(8,128)(2,1)}, u32[]{:S(2)}) copy-start(bf16[7168,256]{1,0:T(8,128)(2,1)} %pad_maximum_fusion) | copy-start | bytes 11010052
Sparse Core Ops, SparseCore 0:
  49.9 81.2 all-gather.1
  151.6 76.7 reduce-scatter.1

commit v4 on v3

--- a/solution.py
+++ b/solution.py
@@ -1,6 +1,7 @@
 import jax
 import jax.numpy as jnp
 from jax import lax
+from jax.sharding import Mesh
 from jax.sharding import PartitionSpec as P
 
 QBLOCK = 128
@@ -82,7 +83,8 @@
     hid = wgate.shape[1]
     wboth = jnp.concatenate([wgate, wup], axis=1)
     wboth_ext = jnp.pad(wboth, ((0, LANE), (0, 0)))
-    gathered = lax.all_gather(recv, "blk", axis=0, tiled=True)
+    gathered = lax.all_gather(recv, "chip", axis=0, tiled=True)
+    gathered = lax.all_gather(gathered, "core", axis=0, tiled=True)
     feats = gathered[:, :width]
     cotan = gathered[:, width : 2 * width]
     gates = gathered[:, 2 * width].astype(jnp.float32)
@@ -98,7 +100,8 @@
     scores = jnp.sum(hidden * down_back, axis=1).astype(jnp.bfloat16).astype(jnp.float32)
     column = lax.broadcasted_iota(jnp.int32, back.shape, 1)
     partial_rows = jnp.where(column == width, scores[:, None], back).astype(jnp.bfloat16)
-    summed = lax.psum_scatter(partial_rows, "blk", scatter_dimension=0, tiled=True)
+    summed = lax.psum_scatter(partial_rows, "core", scatter_dimension=0, tiled=True)
+    summed = lax.psum_scatter(summed, "chip", scatter_dimension=0, tiled=True)
     both_grad = row_sum(feats, grad_both).astype(jnp.bfloat16)
     gate_grad = both_grad[None, :, :hid]
     up_grad = both_grad[None, :, hid:]
@@ -121,23 +124,26 @@
 
 
 def solution(mesh):
+    n_eg, n_blk = mesh.devices.shape
+    split = Mesh(mesh.devices.reshape(n_eg, n_blk // 2, 2), ("eg", "chip", "core"))
+    blk = ("chip", "core")
     in_specs = (
-        P(("eg", "blk"), None),
-        P(("eg", "blk"), None),
-        P(("eg", "blk"), None),
-        P(("eg", "blk"), None),
-        P("eg", None, "blk"),
-        P("eg", None, "blk"),
-        P("eg", None, "blk"),
-        P("eg", None, "blk", None),
+        P(("eg",) + blk, None),
+        P(("eg",) + blk, None),
+        P(("eg",) + blk, None),
+        P(("eg",) + blk, None),
+        P("eg", None, blk),
+        P("eg", None, blk),
+        P("eg", None, blk),
+        P("eg", None, blk, None),
     )
     out_specs = (
-        P(("eg", "blk"), None),
-        P(("eg", "blk"), None),
-        P("eg", None, "blk"),
-        P("eg", None, "blk"),
-        P("eg", None, "blk"),
+        P(("eg",) + blk, None),
+        P(("eg",) + blk, None),
+        P("eg", None, blk),
+        P("eg", None, blk),
+        P("eg", None, blk),
     )
     return jax.shard_map(
-        on_device, mesh=mesh, in_specs=in_specs, out_specs=out_specs, check_vma=False
+        on_device, mesh=split, in_specs=in_specs, out_specs=out_specs, check_vma=False
     )

time: 261 us -> 297 us (1.14)
  waiting for transfers between devices: 133 us -> 168 us
    all_gather x1 -> x2, waiting for transfers between devices: 69.4 us -> 103 us  [the longest x1 81.7 us: on_device(): gathered = lax.all_gather(recv, 'chip', axis=0, tiled=True)]
    reduce_scatter x1 -> x2, waiting for transfers between devices: 63.1 us -> 64.9 us  [the longest x1 42 us: on_device(): summed = lax.psum_scatter(summed, 'chip', scatter_dimension=0, tiled=True)]
  transfers between devices with their start and end apart: 2 -> 4, of which waited for: 2 -> 4; matrix products, arithmetic and copies ran while one was open for 9% -> 8% of each run, Pallas kernels for 0% -> 0%
where the time goes in v4:
time: 297 us
  waiting for transfers between devices  168 us (57%)
  blocking collectives  59.5 us (20%)
  matrix products  33 us (11%)
  between operations  13.9 us (5%)
  other arithmetic  13 us (4%)
  local copies, waits for them, and re-layouts  8.75 us (3%)
    all_gather x1, waiting for transfers between devices, on_device(): gathered = lax.all_gather(recv, 'chip', axis=0, tiled=True)  81.7 us
    reduce_scatter x1, waiting for transfers between devices, on_device(): summed = lax.psum_scatter(summed, 'chip', scatter_dimension=0, tiled=True)  42 us
    all_to_all x1, blocking collectives, on_device(): recv = lax.all_to_all(send, 'eg', split_axis=0, concat_axis=0, tiled=True)  36.3 us
    all_to_all x1, blocking collectives, on_device(): home = lax.all_to_all(summed, 'eg', split_axis=0, concat_axis=0, tiled=True)  23.2 us
    reduce_scatter x1, waiting for transfers between devices, on_device(): lax.psum_scatter(partial_rows, 'core', scatter_dimension=0, tiled=True)  22.9 us
    all_gather x1, waiting for transfers between devices, on_device(): gathered = lax.all_gather(gathered, 'core', axis=0, tiled=True)  21.6 us
    dot_general x2, matrix products, row_sum(): lax.dot_general(left, right, (((0,), (0,)), ((), ())), preferred_element_...  11.7 us
    convert_element_type x2, other arithmetic, dequantize(): return scaled.reshape(rows_in, cols_in).astype(jnp.bfloat16)  7.16 us
  transfers between devices with their start and end apart: 4, of which 4 were waited for; matrix products, arithmetic and copies ran while one was open for 8% of the time, Pallas kernels for 0%

profile of v4, /device:TPU:32, one launch (start us, length us, event | category | flops | bytes accessed | tf_op | source)
XLA Modules:
  0.0 296.9 jit_solution(13479485859994847133)
XLA Ops:
  7.2 0.0 all-gather.3.cloned.1.call-start
  7.2 0.8 fusion.29
  8.0 0.7 fusion.22
  8.7 0.7 bitcast_convert_fusion.4
  9.4 0.1 copy.52
  9.5 0.1 copy.29
  9.6 0.1 multiply_reduce_fusion.2
  9.8 0.1 copy.56
  9.8 0.1 copy.30
  10.0 1.4 convolution_convert_fusion
  11.4 0.1 fusion.16
  11.4 0.7 copy.31
  12.2 36.3 %all_to_all.10 = bf16[16,2,14464]{2,1,0:T(2,128)(2,1)S(1)} all-to-all(bf16[16,2,14464]{2,1,0:T(2,128)(2,1)S(1)} %copy.31), channel_id=1, replica_groups=mesh['eg'=16,'chip'=8,'core'=2] {'eg'}, dimensions={0} | all-to-all | bytes 1851392 | tf_op jit(solution)/shard_map/all_to_all | solution.py:78
  48.5 1.3 reshape.105
  49.7 0.0 all-gather.3.cloned.1.call-update
  49.8 0.0 all-gather.5.cloned.1.call-start
  49.8 81.7 %all-gather.3.cloned.1.call-done = bf16[256,14464]{1,0:T(8,128)(2,1)} async-done(((bf16[32,14464]{1,0:T(8,128)(2,1)}), bf16[256,14464]{1,0:T(8,128)(2,1)}) %all-gather.3.cloned.1.call-update) | async-done | bytes 7405584 | tf_op jit(solution)/shard_map/all_gather | solution.py:86
  131.6 0.0 all-gather.5.cloned.1.call-update
  131.6 0.0 reduce-scatter.3.cloned.1.call-start
  131.6 0.0 copy-start.2
  131.7 0.6 copy-done.3
  132.2 0.1 broadcast_bitcast_fusion
  132.3 0.1 broadcast_bitcast_fusion.1
  132.4 4.2 %fusion.10 = bf16[7168,128]{1,0:T(8,128)(2,1)S(1)} fusion(bf16[1,7168,128]{2,1,0:T(8,128)(2,1)} %param.13, f32[7168]{0:T(1024)S(1)} %get-tuple-element.21), kind=kLoop, calls=%fused_computation.18 | loop fusion | flops 2752512 | bytes 3698688 | tf_op jit(solution)/shard_map/convert_element_type | solution.py:16
  136.6 3.0 %fusion.11 = bf16[7168,128]{1,0:T(8,128)(2,1)S(1)} fusion(bf16[1,7168,128]{2,1,0:T(8,128)(2,1)S(1)} %copy-done.2, f32[7168]{0:T(1024)S(1)} %get-tuple-element.22), kind=kLoop, calls=%fused_computation.20 | loop fusion | flops 2752512 | bytes 3698688 | tf_op jit(solution)/shard_map/convert_element_type | solution.py:16
  139.6 1.2 copy-done
  140.8 2.3 pad_maximum_fusion
  143.1 21.6 %all-gather.5.cloned.1.call-done = bf16[512,14464]{1,0:T(8,128)(2,1)} async-done(((bf16[256,14464]{1,0:T(8,128)(2,1)}), bf16[512,14464]{1,0:T(8,128)(2,1)}) %all-gather.5.cloned.1.call-update) | async-done | bytes 14811152 | tf_op jit(solution)/shard_map/all_gather | solution.py:87
  164.7 1.0 convert_reduce_fusion
  165.8 5.9 %fusion.6 = f32[512,256]{0,1:T(8,128)S(1)} fusion(bf16[512,14464]{1,0:T(8,128)(2,1)} %all-gather.5.cloned.1.call-done, bf16[7168,128]{1,0:T(8,128)(2,1)S(1)} %fusion.10, bf16[7168,128]{1,0:T(8,128)(2,1)} %copy-done), kind=kOutput, calls=%fused_computation.11 | convolution fusion | flops 1886388224 | bytes 11534336 | tf_op jit(solution)/shard_map/dot_general | solution.py:91
  171.6 7.0 %multiply_convert_fusion.2 = (bf16[512,128]{0,1:T(8,128)(2,1)S(1)}, bf16[512,128]{0,1:T(8,128)(2,1)S(1)}, bf16[512]{0:T(512)(128)(2,1)S(1)}) fusion(f32[512,256]{0,1:T(8,128)S(1)} %fusion.6, f32[512]{0:T(512)S(1)} %convert_reduce_fusion, bf16[1,7168,128]{2,1,0:T(8,128)(2,1)S(1)} %copy-done.4, f32[7168]{0:T(1024)S(1)} %broadcast_bitcast_fusion, ...), kind=kOutput, calls=%fused_computation.33 | convolution fusion | flops 943455744 | bytes 9993216 | tf_op jit(solution)/shard_map/dot_general | solution.py:94
  178.6 6.2 %select_convert_fusion = bf16[512,7296]{1,0:T(8,128)(2,1)} fusion(bf16[512]{0:T(512)(128)(2,1)S(1)} %get-tuple-element.17, pred[7296]{0:T(1024)(128)(4,1)S(1)} %iota_compare_fusion.1, bf16[7168,256]{1,0:T(8,128)(2,1)S(1)} %copy-done.1, bf16[512,128]{0,1:T(8,128)(2,1)S(1)} %get-tuple-element.16, bf16[512,128]{0,1:T(8,128)(2,1)S(1)} %get-tuple-element.15), kind=kOutput, calls=%fused_computation.1 | convolution fusion | flops 1916862464 | bytes 11411584 | tf_op jit(solution)/shard_map/dot_general | solution.py:97
  184.8 0.0 reduce-scatter.3.cloned.1.call-update
  184.8 0.2 reduce-scatter.5.cloned.1.call-start
  185.0 22.9 %reduce-scatter.3.cloned.1.call-done = bf16[256,7296]{1,0:T(8,128)(2,1)} async-done(((bf16[512,7296]{1,0:T(8,128)(2,1)}), bf16[256,7296]{1,0:T(8,128)(2,1)}) %reduce-scatter.3.cloned.1.call-update) | async-done | bytes 3735568 | tf_op jit(solution)/shard_map/reduce_scatter | solution.py:103
  208.0 0.0 reduce-scatter.5.cloned.1.call-update
  208.0 6.5 %fusion = bf16[1,7168,128]{2,1,0:T(8,128)(2,1)} fusion(bf16[512,14464]{1,0:T(8,128)(2,1)} %all-gather.5.cloned.1.call-done, f32[512]{0:T(512)S(1)} %convert_reduce_fusion, f32[512,256]{0,1:T(8,128)S(1)} %fusion.6), kind=kOutput, calls=%fused_computation.4 | convolution fusion | flops 940900352 | bytes 9701376 | tf_op jit(solution)/shard_map/dot_general | solution.py:56
  214.5 5.2 %convolution_convert_fusion.1 = bf16[7168,256]{1,0:T(8,128)(2,1)S(1)} fusion(bf16[512,14464]{1,0:T(8,128)(2,1)} %all-gather.5.cloned.1.call-done, bf16[512,128]{0,1:T(8,128)(2,1)S(1)} %get-tuple-element.16, bf16[512,128]{0,1:T(8,128)(2,1)S(1)} %get-tuple-element.15), kind=kOutput, calls=%fused_computation.2 | convolution fusion | flops 1881407488 | bytes 11272192 | tf_op jit(solution)/shard_map/dot_general | solution.py:56
  219.7 2.1 slice_bitcast_fusion
  221.8 42.0 %reduce-scatter.5.cloned.1.call-done = bf16[32,7296]{1,0:T(8,128)(2,1)} async-done(((bf16[256,7296]{1,0:T(8,128)(2,1)}), bf16[32,7296]{1,0:T(8,128)(2,1)}) %reduce-scatter.5.cloned.1.call-update) | async-done | bytes 466960 | tf_op jit(solution)/shard_map/reduce_scatter | solution.py:104
  263.8 1.2 reshape.106
  265.0 23.2 %all_to_all.11 = bf16[16,2,7296]{2,1,0:T(2,128)(2,1)S(1)} all-to-all(bf16[16,2,7296]{2,1,0:T(2,128)(2,1)S(1)} %reshape.106), channel_id=1, replica_groups=mesh['eg'=16,'chip'=8,'core'=2] {'eg'}, dimensions={0} | all-to-all | bytes 933888 | tf_op jit(solution)/shard_map/all_to_all | solution.py:113
  288.2 0.3 slice.55
  288.5 0.9 fusion.1
  289.4 0.1 copy.50
  289.5 0.1 copy.53
  289.6 0.2 multiply_reduce_fusion.1
  289.8 0.6 copy.49
  (15 shorter events, 0.1 us)
Async XLA Ops:
  7.2 124.4 %all-gather.3.cloned.1.call-start = ((), (), s32[]{:S(2)}) async-start(), calls=%async_computation.4 | async-start | bytes 8331264 | tf_op jit(solution)/shard_map/all_gather | solution.py:86
  49.8 115.0 %all-gather.5.cloned.1.call-start = ((), (), s32[]{:S(2)}) async-start(), calls=%async_computation.5 | async-start | bytes 22216704 | tf_op jit(solution)/shard_map/all_gather | solution.py:87
  131.6 0.7 copy-start.3
  131.6 76.4 %reduce-scatter.3.cloned.1.call-start = ((), (), s32[]{:S(2)}) async-start(), calls=%async_computation.6 | async-start | bytes 11206656 | tf_op jit(solution)/shard_map/reduce_scatter | solution.py:103
  131.6 4.9 %copy-start.2 = (bf16[1,7168,128]{2,1,0:T(8,128)(2,1)S(1)}, bf16[1,7168,128]{2,1,0:T(8,128)(2,1)}, u32[]{:S(2)}) copy-start(bf16[1,7168,128]{2,1,0:T(8,128)(2,1)} %param.12) | copy-start | bytes 5505028
  139.6 1.2 copy-start
  165.7 5.9 %copy-start.4 = (bf16[1,7168,128]{2,1,0:T(8,128)(2,1)S(1)}, bf16[1,7168,128]{2,1,0:T(8,128)(2,1)}, u32[]{:S(2)}) copy-start(bf16[1,7168,128]{2,1,0:T(8,128)(2,1)} %param.14) | copy-start | bytes 5505028
  171.6 7.0 %copy-start.1 = (bf16[7168,256]{1,0:T(8,128)(2,1)S(1)}, bf16[7168,256]{1,0:T(8,128)(2,1)}, u32[]{:S(2)}) copy-start(bf16[7168,256]{1,0:T(8,128)(2,1)} %pad_maximum_fusion) | copy-start | bytes 11010052
  184.8 79.0 %reduce-scatter.5.cloned.1.call-start = ((), (), s32[]{:S(2)}) async-start(), calls=%async_computation.7 | async-start | bytes 4202496 | tf_op jit(solution)/shard_map/reduce_scatter | solution.py:104
Sparse Core Ops, SparseCore 0:
  49.9 81.6 all-gather.2
  133.4 31.3 all-gather.4
  184.9 23.0 reduce-scatter.2
  210.4 53.3 reduce-scatter.4

commit v5 on v4

--- a/solution.py
+++ b/solution.py
@@ -7,6 +7,7 @@
 QBLOCK = 128
 TOPK = 2
 LANE = 128
+BLK = ("chip", "core")
 
 
 def dequantize(codes, scales):
@@ -83,8 +84,7 @@
     hid = wgate.shape[1]
     wboth = jnp.concatenate([wgate, wup], axis=1)
     wboth_ext = jnp.pad(wboth, ((0, LANE), (0, 0)))
-    gathered = lax.all_gather(recv, "chip", axis=0, tiled=True)
-    gathered = lax.all_gather(gathered, "core", axis=0, tiled=True)
+    gathered = lax.all_gather(recv, BLK, axis=0, tiled=True)
     feats = gathered[:, :width]
     cotan = gathered[:, width : 2 * width]
     gates = gathered[:, 2 * width].astype(jnp.float32)
@@ -100,8 +100,15 @@
     scores = jnp.sum(hidden * down_back, axis=1).astype(jnp.bfloat16).astype(jnp.float32)
     column = lax.broadcasted_iota(jnp.int32, back.shape, 1)
     partial_rows = jnp.where(column == width, scores[:, None], back).astype(jnp.bfloat16)
-    summed = lax.psum_scatter(partial_rows, "core", scatter_dimension=0, tiled=True)
-    summed = lax.psum_scatter(summed, "chip", scatter_dimension=0, tiled=True)
+    chips = lax.axis_size("chip")
+    core = lax.axis_index("core")
+    by_core = partial_rows.reshape(chips, 2, -1, partial_rows.shape[1])
+    mine = jnp.where(core == 0, by_core[:, 0], by_core[:, 1])
+    theirs = jnp.where(core == 0, by_core[:, 1], by_core[:, 0])
+    swapped = lax.ppermute(theirs, "core", [(0, 1), (1, 0)])
+    pair = (mine.astype(jnp.float32) + swapped.astype(jnp.float32)).astype(jnp.bfloat16)
+    pair = pair.reshape(-1, partial_rows.shape[1])
+    summed = lax.psum_scatter(pair, "chip", scatter_dimension=0, tiled=True)
     both_grad = row_sum(feats, grad_both).astype(jnp.bfloat16)
     gate_grad = both_grad[None, :, :hid]
     up_grad = both_grad[None, :, hid:]
@@ -125,24 +132,23 @@
 
 def solution(mesh):
     n_eg, n_blk = mesh.devices.shape
-    split = Mesh(mesh.devices.reshape(n_eg, n_blk // 2, 2), ("eg", "chip", "core"))
-    blk = ("chip", "core")
+    split = Mesh(mesh.devices.reshape(n_eg, n_blk // 2, 2), ("eg",) + BLK)
     in_specs = (
-        P(("eg",) + blk, None),
-        P(("eg",) + blk, None),
-        P(("eg",) + blk, None),
-        P(("eg",) + blk, None),
-        P("eg", None, blk),
-        P("eg", None, blk),
-        P("eg", None, blk),
-        P("eg", None, blk, None),
+        P(("eg",) + BLK, None),
+        P(("eg",) + BLK, None),
+        P(("eg",) + BLK, None),
+        P(("eg",) + BLK, None),
+        P("eg", None, BLK),
+        P("eg", None, BLK),
+        P("eg", None, BLK),
+        P("eg", None, BLK, None),
     )
     out_specs = (
-        P(("eg",) + blk, None),
-        P(("eg",) + blk, None),
-        P("eg", None, blk),
-        P("eg", None, blk),
-        P("eg", None, blk),
+        P(("eg",) + BLK, None),
+        P(("eg",) + BLK, None),
+        P("eg", None, BLK),
+        P("eg", None, BLK),
+        P("eg", None, BLK),
     )
     return jax.shard_map(
         on_device, mesh=split, in_specs=in_specs, out_specs=out_specs, check_vma=False

time: 297 us -> 245 us (0.82)
  waiting for transfers between devices: 168 us -> 115 us
  other arithmetic: 13 us -> 17.1 us
  matrix products: 33 us -> 30 us
    all_gather x2 -> x1, waiting for transfers between devices: 103 us -> 69.4 us  [on_device(): gathered = lax.all_gather(recv, BLK, axis=0, tiled=True)]
    reduce_scatter x2 -> x1, waiting for transfers between devices: 64.9 us -> 39.4 us  [on_device(): summed = lax.psum_scatter(pair, 'chip', scatter_dimension=0, tiled=True)]
    ppermute x0 -> x1, waiting for transfers between devices: none -> 6.25 us  [on_device(): swapped = lax.ppermute(theirs, 'core', [(0, 1), (1, 0)])]
  transfers between devices with their start and end apart: 4 -> 3, of which waited for: 4 -> 3; matrix products, arithmetic and copies ran while one was open for 8% -> 10% of each run, Pallas kernels for 0% -> 0%
where the time goes in v5:
time: 245 us
  waiting for transfers between devices  115 us (47%)
  blocking collectives  59.4 us (24%)
  matrix products  30 us (12%)
  other arithmetic  17.1 us (7%)
  between operations  14.2 us (6%)
  local copies, waits for them, and re-layouts  8.17 us (3%)
    all_gather x1, waiting for transfers between devices, on_device(): gathered = lax.all_gather(recv, BLK, axis=0, tiled=True)  69.4 us
    reduce_scatter x1, waiting for transfers between devices, on_device(): summed = lax.psum_scatter(pair, 'chip', scatter_dimension=0, tiled=True)  39.4 us
    all_to_all x1, blocking collectives, on_device(): recv = lax.all_to_all(send, 'eg', split_axis=0, concat_axis=0, tiled=True)  36.3 us
    all_to_all x1, blocking collectives, on_device(): home = lax.all_to_all(summed, 'eg', split_axis=0, concat_axis=0, tiled=True)  23.1 us
    dot_general x2, matrix products, row_sum(): lax.dot_general(left, right, (((0,), (0,)), ((), ())), preferred_element_...  11.7 us
    convert_element_type x2, other arithmetic, dequantize(): return scaled.reshape(rows_in, cols_in).astype(jnp.bfloat16)  8.32 us
    dot_general x1, matrix products, on_device(): down_back = jnp.dot(cotan, wdown, preferred_element_type=jnp.float32)  6.98 us
    ppermute x1, waiting for transfers between devices, on_device(): swapped = lax.ppermute(theirs, 'core', [(0, 1), (1, 0)])  6.25 us
  transfers between devices with their start and end apart: 3, of which 3 were waited for; matrix products, arithmetic and copies ran while one was open for 10% of the time, Pallas kernels for 0%

profile of v5, /device:TPU:32, one launch (start us, length us, event | category | flops | bytes accessed | tf_op | source)
XLA Modules:
  0.0 244.7 jit_solution(8260862561029181690)
XLA Ops:
  7.2 0.0 all-gather.2.cloned.1.call-start
  7.2 0.8 fusion.32
  8.0 0.7 fusion.25
  8.7 0.7 bitcast_convert_fusion.4
  9.4 0.1 copy.68
  9.5 0.1 copy.40
  9.6 0.1 multiply_reduce_fusion.2
  9.8 0.1 copy.72
  9.8 0.1 copy.41
  10.0 1.4 convolution_convert_fusion
  11.4 0.1 fusion.19
  11.4 0.0 copy-start.2
  11.4 0.7 copy.42
  12.2 36.3 %all_to_all.10 = bf16[16,2,14464]{2,1,0:T(2,128)(2,1)S(1)} all-to-all(bf16[16,2,14464]{2,1,0:T(2,128)(2,1)S(1)} %copy.42), channel_id=1, replica_groups=mesh['eg'=16,'chip'=8,'core'=2] {'eg'}, dimensions={0} | all-to-all | bytes 1851392 | tf_op jit(solution)/shard_map/all_to_all | solution.py:79
  48.5 1.3 reshape.117
  49.7 0.0 all-gather.2.cloned.1.call-update
  49.8 0.0 reduce-scatter.2.cloned.1.call-start
  49.9 0.1 broadcast_bitcast_fusion.2
  49.9 0.1 broadcast_bitcast_fusion
  50.0 4.2 %fusion.14 = bf16[7168,128]{1,0:T(8,128)(2,1)S(1)} fusion(bf16[1,7168,128]{2,1,0:T(8,128)(2,1)} %param.12, f32[7168]{0:T(1024)S(1)} %broadcast_bitcast_fusion.2), kind=kLoop, calls=%fused_computation.26 | loop fusion | flops 2752512 | bytes 3698688 | tf_op jit(solution)/shard_map/convert_element_type | solution.py:17
  54.2 4.2 %fusion.13 = bf16[7168,128]{1,0:T(8,128)(2,1)S(1)} fusion(bf16[1,7168,128]{2,1,0:T(8,128)(2,1)} %param.13, f32[7168]{0:T(1024)S(1)} %get-tuple-element.22), kind=kLoop, calls=%fused_computation.24 | loop fusion | flops 2752512 | bytes 3698688 | tf_op jit(solution)/shard_map/convert_element_type | solution.py:17
  58.3 0.0 copy-start
  58.4 1.2 copy-done
  59.6 2.2 pad_maximum_fusion
  61.8 69.4 %all-gather.2.cloned.1.call-done = bf16[512,14464]{1,0:T(8,128)(2,1)} async-done(((bf16[32,14464]{1,0:T(8,128)(2,1)}), bf16[512,14464]{1,0:T(8,128)(2,1)}) %all-gather.2.cloned.1.call-update) | async-done | bytes 14811152 | tf_op jit(solution)/shard_map/all_gather | solution.py:87
  131.2 1.0 convert_reduce_fusion
  132.2 0.0 copy-start.3
  132.2 5.8 %fusion.7 = f32[512,256]{0,1:T(8,128)S(1)} fusion(bf16[512,14464]{1,0:T(8,128)(2,1)} %all-gather.2.cloned.1.call-done, bf16[7168,128]{1,0:T(8,128)(2,1)} %copy-done, bf16[7168,128]{1,0:T(8,128)(2,1)S(1)} %fusion.14), kind=kOutput, calls=%fused_computation.14 | convolution fusion | flops 1886388224 | bytes 11534336 | tf_op jit(solution)/shard_map/dot_general | solution.py:91
  138.1 7.0 %multiply_convert_fusion.2 = (bf16[512,128]{0,1:T(8,128)(2,1)S(1)}, bf16[512,128]{0,1:T(8,128)(2,1)S(1)}, bf16[512]{0:T(512)(128)(2,1)S(1)}) fusion(f32[512,256]{0,1:T(8,128)S(1)} %fusion.7, f32[512]{0:T(512)S(1)} %convert_reduce_fusion, bf16[1,7168,128]{2,1,0:T(8,128)(2,1)S(1)} %copy-done.3, f32[7168]{0:T(1024)S(1)} %get-tuple-element.21, ...), kind=kOutput, calls=%fused_computation.39 | convolution fusion | flops 943455744 | bytes 9993216 | tf_op jit(solution)/shard_map/dot_general | solution.py:94
  145.1 0.0 copy-done.1
  145.1 3.2 %select_convert_fusion = bf16[512,7296]{1,0:T(8,128)(2,1)S(1)} fusion(bf16[512]{0:T(512)(128)(2,1)S(1)} %get-tuple-element.17, pred[7296]{0:T(1024)(128)(4,1)S(1)} %iota_compare_fusion.1, bf16[7168,256]{1,0:T(8,128)(2,1)S(1)} %copy-done.1, bf16[512,128]{0,1:T(8,128)(2,1)S(1)} %get-tuple-element.16, bf16[512,128]{0,1:T(8,128)(2,1)S(1)} %get-tuple-element.15), kind=kOutput, calls=%fused_computation.1 | convolution fusion | flops 1916862464 | bytes 11411584 | tf_op jit(solution)/shard_map/dot_general | solution.py:97
  148.3 0.4 fusion.9
  148.7 0.5 collective-permute-start
  149.2 6.3 %collective-permute-done = bf16[8,32,7296]{2,1,0:T(8,128)(2,1)S(1)} collective-permute-done((bf16[8,32,7296]{2,1,0:T(8,128)(2,1)S(1)}, bf16[8,32,7296]{2,1,0:T(8,128)(2,1)S(1)}, u32[]{:S(2)}, u32[]{:S(2)}) %collective-permute-start) | collective-permute-done | bytes 3735584 | tf_op jit(solution)/shard_map/ppermute | solution.py:108
  155.5 2.6 %fusion.2 = bf16[8,32,7296]{2,1,0:T(8,128)(2,1)} fusion(bf16[8,32,7296]{2,1,0:T(8,128)(2,1)S(1)} %collective-permute-done, pred[]{:T(512)S(6)} %eq.51, bf16[8,2,32,7296]{3,2,1,0:T(8,128)(2,1)S(1)} %bitcast.78), kind=kLoop, calls=%fused_computation.8 | loop fusion | flops 9338880 | bytes 14942209 | tf_op jit(solution)/shard_map/convert_element_type | solution.py:109
  158.1 0.0 reduce-scatter.2.cloned.1.call-update
  158.1 6.5 %fusion = bf16[1,7168,128]{2,1,0:T(8,128)(2,1)} fusion(bf16[512,14464]{1,0:T(8,128)(2,1)} %all-gather.2.cloned.1.call-done, f32[512]{0:T(512)S(1)} %convert_reduce_fusion, f32[512,256]{0,1:T(8,128)S(1)} %fusion.7), kind=kOutput, calls=%fused_computation.4 | convolution fusion | flops 940900352 | bytes 9701376 | tf_op jit(solution)/shard_map/dot_general | solution.py:57
  164.6 5.2 %convolution_convert_fusion.1 = bf16[7168,256]{1,0:T(8,128)(2,1)S(1)} fusion(bf16[512,14464]{1,0:T(8,128)(2,1)} %all-gather.2.cloned.1.call-done, bf16[512,128]{0,1:T(8,128)(2,1)S(1)} %get-tuple-element.16, bf16[512,128]{0,1:T(8,128)(2,1)S(1)} %get-tuple-element.15), kind=kOutput, calls=%fused_computation.2 | convolution fusion | flops 1881407488 | bytes 11272192 | tf_op jit(solution)/shard_map/dot_general | solution.py:57
  169.8 2.1 slice_bitcast_fusion
  171.9 39.4 %reduce-scatter.2.cloned.1.call-done = bf16[32,7296]{1,0:T(8,128)(2,1)} async-done(((bf16[256,7296]{1,0:T(8,128)(2,1)}), bf16[32,7296]{1,0:T(8,128)(2,1)}) %reduce-scatter.2.cloned.1.call-update) | async-done | bytes 466960 | tf_op jit(solution)/shard_map/reduce_scatter | solution.py:111
  211.4 1.2 reshape.120
  212.6 23.1 %all_to_all.11 = bf16[16,2,7296]{2,1,0:T(2,128)(2,1)S(1)} all-to-all(bf16[16,2,7296]{2,1,0:T(2,128)(2,1)S(1)} %reshape.120), channel_id=1, replica_groups=mesh['eg'=16,'chip'=8,'core'=2] {'eg'}, dimensions={0} | all-to-all | bytes 933888 | tf_op jit(solution)/shard_map/all_to_all | solution.py:120
  235.7 0.3 slice.67
  236.0 0.9 fusion.1
  236.9 0.1 copy.65
  237.0 0.1 copy.69
  237.1 0.2 multiply_reduce_fusion.1
  237.3 0.6 copy.64
  (11 shorter events, 0.1 us)
Async XLA Ops:
  7.2 124.0 %all-gather.2.cloned.1.call-start = ((), (), s32[]{:S(2)}) async-start(), calls=%async_computation.3 | async-start | bytes 15736832 | tf_op jit(solution)/shard_map/all_gather | solution.py:87
  11.4 38.4 %copy-start.2 = (bf16[1,3,1,56]{3,1,2,0:T(4,128)(2,1)S(1)}, bf16[1,3,1,56]{3,1,2,0:T(4,128)(2,1)}, u32[]{:S(2)}) copy-start(bf16[1,3,1,56]{3,1,2,0:T(4,128)(2,1)} %param.15) | copy-start | bytes 1012
  49.8 161.6 %reduce-scatter.2.cloned.1.call-start = ((), (), s32[]{:S(2)}) async-start(), calls=%async_computation.4 | async-start | bytes 4202496 | tf_op jit(solution)/shard_map/reduce_scatter | solution.py:111
  58.3 1.2 copy-start
  132.2 5.9 %copy-start.3 = (bf16[1,7168,128]{2,1,0:T(8,128)(2,1)S(1)}, bf16[1,7168,128]{2,1,0:T(8,128)(2,1)}, u32[]{:S(2)}) copy-start(bf16[1,7168,128]{2,1,0:T(8,128)(2,1)} %param.14) | copy-start | bytes 5505028
  138.1 7.0 %copy-start.1 = (bf16[7168,256]{1,0:T(8,128)(2,1)S(1)}, bf16[7168,256]{1,0:T(8,128)(2,1)}, u32[]{:S(2)}) copy-start(bf16[7168,256]{1,0:T(8,128)(2,1)} %pad_maximum_fusion) | copy-start | bytes 11010052
  148.7 6.8 %collective-permute-start = (bf16[8,32,7296]{2,1,0:T(8,128)(2,1)S(1)}, bf16[8,32,7296]{2,1,0:T(8,128)(2,1)S(1)}, u32[]{:S(2)}, u32[]{:S(2)}) collective-permute-start(bf16[8,32,7296]{2,1,0:T(8,128)(2,1)S(1)} %fusion.9), channel_id=1, source_target_pairs={{0,1},{1,0},{2,3},{3,2},{4,5},{5,4},{6,7},{7,6},{8,9},{9,8},{10,11... | collective-permute-start | bytes 11206664 | tf_op jit(solution)/shard_map/ppermute | solution.py:108
Sparse Core Ops, SparseCore 0:
  49.9 81.2 all-gather.1
  158.3 53.0 reduce-scatter.1

commit v6 on v5

--- a/solution.py
+++ b/solution.py
@@ -106,13 +106,14 @@
     mine = jnp.where(core == 0, by_core[:, 0], by_core[:, 1])
     theirs = jnp.where(core == 0, by_core[:, 1], by_core[:, 0])
     swapped = lax.ppermute(theirs, "core", [(0, 1), (1, 0)])
+    down_grad = row_sum(cotan, gated_hidden).astype(jnp.bfloat16)[None]
+    swapped, down_grad = lax.optimization_barrier((swapped, down_grad))
     pair = (mine.astype(jnp.float32) + swapped.astype(jnp.float32)).astype(jnp.bfloat16)
     pair = pair.reshape(-1, partial_rows.shape[1])
     summed = lax.psum_scatter(pair, "chip", scatter_dimension=0, tiled=True)
     both_grad = row_sum(feats, grad_both).astype(jnp.bfloat16)
     gate_grad = both_grad[None, :, :hid]
     up_grad = both_grad[None, :, hid:]
-    down_grad = row_sum(cotan, gated_hidden).astype(jnp.bfloat16)[None]
     summed, gate_grad, up_grad, down_grad = lax.optimization_barrier(
         (summed, gate_grad, up_grad, down_grad)
     )

time: 245 us -> 245 us (level)
    reduce_scatter x1, waiting for transfers between devices: 39.4 us -> 46 us  [on_device(): summed = lax.psum_scatter(pair, 'chip', scatter_dimension=0, tiled=True)]
    ppermute x1, waiting for transfers between devices: 6.25 us -> 0.01 us  [on_device(): swapped = lax.ppermute(theirs, 'core', [(0, 1), (1, 0)])]
  transfers between devices with their start and end apart: 3 -> 3, of which waited for: 3 -> 2; matrix products, arithmetic and copies ran while one was open for 10% -> 10% of each run, Pallas kernels for 0% -> 0%
where the time goes in v6:
time: 245 us
  waiting for transfers between devices  115 us (47%)
  blocking collectives  59.4 us (24%)
  matrix products  30 us (12%)
  other arithmetic  17.2 us (7%)
  between operations  14.2 us (6%)
  local copies, waits for them, and re-layouts  8.17 us (3%)
    all_gather x1, waiting for transfers between devices, on_device(): gathered = lax.all_gather(recv, BLK, axis=0, tiled=True)  69.4 us
    reduce_scatter x1, waiting for transfers between devices, on_device(): summed = lax.psum_scatter(pair, 'chip', scatter_dimension=0, tiled=True)  46 us
    all_to_all x1, blocking collectives, on_device(): recv = lax.all_to_all(send, 'eg', split_axis=0, concat_axis=0, tiled=True)  36.3 us
    all_to_all x1, blocking collectives, on_device(): home = lax.all_to_all(summed, 'eg', split_axis=0, concat_axis=0, tiled=True)  23.1 us
    dot_general x2, matrix products, row_sum(): lax.dot_general(left, right, (((0,), (0,)), ((), ())), preferred_element_...  11.7 us
    convert_element_type x2, other arithmetic, dequantize(): return scaled.reshape(rows_in, cols_in).astype(jnp.bfloat16)  8.32 us
    dot_general x1, matrix products, on_device(): down_back = jnp.dot(cotan, wdown, preferred_element_type=jnp.float32)  6.96 us
    dot_general x1, matrix products, on_device(): both_pre = jnp.dot(feats, wboth, preferred_element_type=jnp.float32)  5.85 us
  transfers between devices with their start and end apart: 3, of which 2 were waited for; matrix products, arithmetic and copies ran while one was open for 10% of the time, Pallas kernels for 0%

profile of v6, /device:TPU:32, one launch (start us, length us, event | category | flops | bytes accessed | tf_op | source)
XLA Modules:
  0.0 245.0 jit_solution(18383591419522546211)
XLA Ops:
  7.2 0.0 all-gather.2.cloned.1.call-start
  7.2 0.8 fusion.32
  8.0 0.7 fusion.25
  8.7 0.7 bitcast_convert_fusion.4
  9.4 0.1 copy.68
  9.5 0.1 copy.40
  9.6 0.1 multiply_reduce_fusion.2
  9.8 0.1 copy.72
  9.8 0.1 copy.41
  10.0 1.4 convolution_convert_fusion
  11.4 0.1 fusion.19
  11.4 0.0 copy-start.2
  11.4 0.7 copy.42
  12.2 36.3 %all_to_all.10 = bf16[16,2,14464]{2,1,0:T(2,128)(2,1)S(1)} all-to-all(bf16[16,2,14464]{2,1,0:T(2,128)(2,1)S(1)} %copy.42), channel_id=1, replica_groups=mesh['eg'=16,'chip'=8,'core'=2] {'eg'}, dimensions={0} | all-to-all | bytes 1851392 | tf_op jit(solution)/shard_map/all_to_all | solution.py:79
  48.5 1.3 reshape.117
  49.7 0.0 all-gather.2.cloned.1.call-update
  49.8 0.0 reduce-scatter.2.cloned.1.call-start
  49.8 0.0 copy-done.2
  49.9 0.1 broadcast_bitcast_fusion.2
  49.9 0.1 broadcast_bitcast_fusion
  50.0 4.2 %fusion.14 = bf16[7168,128]{1,0:T(8,128)(2,1)S(1)} fusion(bf16[1,7168,128]{2,1,0:T(8,128)(2,1)} %param.12, f32[7168]{0:T(1024)S(1)} %broadcast_bitcast_fusion.2), kind=kLoop, calls=%fused_computation.26 | loop fusion | flops 2752512 | bytes 3698688 | tf_op jit(solution)/shard_map/convert_element_type | solution.py:17
  54.2 4.2 %fusion.13 = bf16[7168,128]{1,0:T(8,128)(2,1)S(1)} fusion(bf16[1,7168,128]{2,1,0:T(8,128)(2,1)} %param.13, f32[7168]{0:T(1024)S(1)} %get-tuple-element.26), kind=kLoop, calls=%fused_computation.24 | loop fusion | flops 2752512 | bytes 3698688 | tf_op jit(solution)/shard_map/convert_element_type | solution.py:17
  58.3 0.0 copy-start
  58.4 1.2 copy-done
  59.6 2.2 pad_maximum_fusion
  61.8 69.4 %all-gather.2.cloned.1.call-done = bf16[512,14464]{1,0:T(8,128)(2,1)} async-done(((bf16[32,14464]{1,0:T(8,128)(2,1)}), bf16[512,14464]{1,0:T(8,128)(2,1)}) %all-gather.2.cloned.1.call-update) | async-done | bytes 14811152 | tf_op jit(solution)/shard_map/all_gather | solution.py:87
  131.2 1.0 convert_reduce_fusion
  132.2 0.0 copy-start.3
  132.2 5.8 %fusion.7 = f32[512,256]{0,1:T(8,128)S(1)} fusion(bf16[512,14464]{1,0:T(8,128)(2,1)} %all-gather.2.cloned.1.call-done, bf16[7168,128]{1,0:T(8,128)(2,1)} %copy-done, bf16[7168,128]{1,0:T(8,128)(2,1)S(1)} %fusion.14), kind=kOutput, calls=%fused_computation.14 | convolution fusion | flops 1886388224 | bytes 11534336 | tf_op jit(solution)/shard_map/dot_general | solution.py:91
  138.1 7.0 %multiply_convert_fusion.2 = (bf16[512,128]{0,1:T(8,128)(2,1)S(1)}, bf16[512,128]{0,1:T(8,128)(2,1)S(1)}, bf16[512]{0:T(512)(128)(2,1)S(1)}) fusion(f32[512,256]{0,1:T(8,128)S(1)} %fusion.7, f32[512]{0:T(512)S(1)} %convert_reduce_fusion, bf16[1,7168,128]{2,1,0:T(8,128)(2,1)S(1)} %copy-done.3, f32[7168]{0:T(1024)S(1)} %get-tuple-element.25, ...), kind=kOutput, calls=%fused_computation.39 | convolution fusion | flops 943455744 | bytes 9993216 | tf_op jit(solution)/shard_map/dot_general | solution.py:94
  145.1 3.2 %select_convert_fusion = bf16[512,7296]{1,0:T(8,128)(2,1)S(1)} fusion(bf16[512]{0:T(512)(128)(2,1)S(1)} %get-tuple-element.21, pred[7296]{0:T(1024)(128)(4,1)S(1)} %iota_compare_fusion.1, bf16[7168,256]{1,0:T(8,128)(2,1)S(1)} %copy-done.1, bf16[512,128]{0,1:T(8,128)(2,1)S(1)} %get-tuple-element.20, bf16[512,128]{0,1:T(8,128)(2,1)S(1)} %get-tuple-element.19), kind=kOutput, calls=%fused_computation.1 | convolution fusion | flops 1916862464 | bytes 11411584 | tf_op jit(solution)/shard_map/dot_general | solution.py:97
  148.3 0.4 fusion.9
  148.7 0.5 collective-permute-start
  149.2 6.5 %fusion = bf16[1,7168,128]{2,1,0:T(8,128)(2,1)} fusion(bf16[512,14464]{1,0:T(8,128)(2,1)} %all-gather.2.cloned.1.call-done, f32[512]{0:T(512)S(1)} %convert_reduce_fusion, f32[512,256]{0,1:T(8,128)S(1)} %fusion.7), kind=kOutput, calls=%fused_computation.4 | convolution fusion | flops 940900352 | bytes 9701376 | tf_op jit(solution)/shard_map/dot_general | solution.py:57
  155.7 0.0 collective-permute-done
  155.7 2.6 %fusion.2 = bf16[8,32,7296]{2,1,0:T(8,128)(2,1)} fusion(bf16[8,32,7296]{2,1,0:T(8,128)(2,1)S(1)} %collective-permute-done, pred[]{:T(512)S(6)} %eq.51, bf16[8,2,32,7296]{3,2,1,0:T(8,128)(2,1)S(1)} %bitcast.78), kind=kLoop, calls=%fused_computation.8 | loop fusion | flops 9338880 | bytes 14942209 | tf_op jit(solution)/shard_map/convert_element_type | solution.py:111
  158.3 0.0 reduce-scatter.2.cloned.1.call-update
  158.4 5.2 %convolution_convert_fusion.1 = bf16[7168,256]{1,0:T(8,128)(2,1)S(1)} fusion(bf16[512,14464]{1,0:T(8,128)(2,1)} %all-gather.2.cloned.1.call-done, bf16[512,128]{0,1:T(8,128)(2,1)S(1)} %get-tuple-element.20, bf16[512,128]{0,1:T(8,128)(2,1)S(1)} %get-tuple-element.19), kind=kOutput, calls=%fused_computation.2 | convolution fusion | flops 1881407488 | bytes 11272192 | tf_op jit(solution)/shard_map/dot_general | solution.py:57
  163.6 2.1 slice_bitcast_fusion
  165.7 46.0 %reduce-scatter.2.cloned.1.call-done = bf16[32,7296]{1,0:T(8,128)(2,1)} async-done(((bf16[256,7296]{1,0:T(8,128)(2,1)}), bf16[32,7296]{1,0:T(8,128)(2,1)}) %reduce-scatter.2.cloned.1.call-update) | async-done | bytes 466960 | tf_op jit(solution)/shard_map/reduce_scatter | solution.py:113
  211.6 1.2 reshape.120
  212.8 23.1 %all_to_all.11 = bf16[16,2,7296]{2,1,0:T(2,128)(2,1)S(1)} all-to-all(bf16[16,2,7296]{2,1,0:T(2,128)(2,1)S(1)} %reshape.120), channel_id=1, replica_groups=mesh['eg'=16,'chip'=8,'core'=2] {'eg'}, dimensions={0} | all-to-all | bytes 933888 | tf_op jit(solution)/shard_map/all_to_all | solution.py:121
  235.9 0.3 slice.67
  236.2 0.9 fusion.1
  237.1 0.1 copy.65
  237.2 0.1 copy.69
  237.3 0.2 multiply_reduce_fusion.1
  237.5 0.6 copy.64
  (11 shorter events, 0.1 us)
Async XLA Ops:
  7.2 124.0 %all-gather.2.cloned.1.call-start = ((), (), s32[]{:S(2)}) async-start(), calls=%async_computation.3 | async-start | bytes 15736832 | tf_op jit(solution)/shard_map/all_gather | solution.py:87
  11.4 38.4 %copy-start.2 = (bf16[1,3,1,56]{3,1,2,0:T(4,128)(2,1)S(1)}, bf16[1,3,1,56]{3,1,2,0:T(4,128)(2,1)}, u32[]{:S(2)}) copy-start(bf16[1,3,1,56]{3,1,2,0:T(4,128)(2,1)} %param.15) | copy-start | bytes 1012
  49.8 161.9 %reduce-scatter.2.cloned.1.call-start = ((), (), s32[]{:S(2)}) async-start(), calls=%async_computation.4 | async-start | bytes 4202496 | tf_op jit(solution)/shard_map/reduce_scatter | solution.py:113
  58.3 1.2 copy-start
  132.2 5.9 %copy-start.3 = (bf16[1,7168,128]{2,1,0:T(8,128)(2,1)S(1)}, bf16[1,7168,128]{2,1,0:T(8,128)(2,1)}, u32[]{:S(2)}) copy-start(bf16[1,7168,128]{2,1,0:T(8,128)(2,1)} %param.14) | copy-start | bytes 5505028
  138.1 7.0 %copy-start.1 = (bf16[7168,256]{1,0:T(8,128)(2,1)S(1)}, bf16[7168,256]{1,0:T(8,128)(2,1)}, u32[]{:S(2)}) copy-start(bf16[7168,256]{1,0:T(8,128)(2,1)} %pad_maximum_fusion) | copy-start | bytes 11010052
  148.7 7.0 %collective-permute-start = (bf16[8,32,7296]{2,1,0:T(8,128)(2,1)S(1)}, bf16[8,32,7296]{2,1,0:T(8,128)(2,1)S(1)}, u32[]{:S(2)}, u32[]{:S(2)}) collective-permute-start(bf16[8,32,7296]{2,1,0:T(8,128)(2,1)S(1)} %fusion.9), channel_id=1, source_target_pairs={{0,1},{1,0},{2,3},{3,2},{4,5},{5,4},{6,7},{7,6},{8,9},{9,8},{10,11... | collective-permute-start | bytes 11206664 | tf_op jit(solution)/shard_map/ppermute | solution.py:108
Sparse Core Ops, SparseCore 0:
  49.9 81.2 all-gather.1
  158.5 53.1 reduce-scatter.1

commit v7 on v5

--- a/solution.py
+++ b/solution.py
@@ -84,35 +84,39 @@
     hid = wgate.shape[1]
     wboth = jnp.concatenate([wgate, wup], axis=1)
     wboth_ext = jnp.pad(wboth, ((0, LANE), (0, 0)))
-    gathered = lax.all_gather(recv, BLK, axis=0, tiled=True)
-    feats = gathered[:, :width]
-    cotan = gathered[:, width : 2 * width]
-    gates = gathered[:, 2 * width].astype(jnp.float32)
-    both_pre = jnp.dot(feats, wboth, preferred_element_type=jnp.float32)
-    gate_pre = both_pre[:, :hid]
-    up_pre = both_pre[:, hid:]
-    down_back = jnp.dot(cotan, wdown, preferred_element_type=jnp.float32)
-    hidden, grad_gate, grad_up, gated_hidden = backward_math(gate_pre, up_pre, down_back, gates)
-    grad_both = jnp.concatenate([grad_gate, grad_up], axis=1)
-    back = lax.dot_general(
-        grad_both, wboth_ext, (((1,), (1,)), ((), ())), preferred_element_type=jnp.float32
-    )
-    scores = jnp.sum(hidden * down_back, axis=1).astype(jnp.bfloat16).astype(jnp.float32)
-    column = lax.broadcasted_iota(jnp.int32, back.shape, 1)
-    partial_rows = jnp.where(column == width, scores[:, None], back).astype(jnp.bfloat16)
-    chips = lax.axis_size("chip")
+    gathered = lax.all_gather(recv, ("core", "chip"), axis=0, tiled=True)
+    half = gathered.shape[0] // 2
     core = lax.axis_index("core")
-    by_core = partial_rows.reshape(chips, 2, -1, partial_rows.shape[1])
-    mine = jnp.where(core == 0, by_core[:, 0], by_core[:, 1])
-    theirs = jnp.where(core == 0, by_core[:, 1], by_core[:, 0])
+
+    def rows_of(index):
+        block = lax.dynamic_slice_in_dim(gathered, index * half, half, axis=0)
+        feats = block[:, :width]
+        cotan = block[:, width : 2 * width]
+        gates = block[:, 2 * width].astype(jnp.float32)
+        both_pre = jnp.dot(feats, wboth, preferred_element_type=jnp.float32)
+        down_back = jnp.dot(cotan, wdown, preferred_element_type=jnp.float32)
+        hidden, grad_gate, grad_up, gated_hidden = backward_math(
+            both_pre[:, :hid], both_pre[:, hid:], down_back, gates
+        )
+        grad_both = jnp.concatenate([grad_gate, grad_up], axis=1)
+        back = lax.dot_general(
+            grad_both, wboth_ext, (((1,), (1,)), ((), ())), preferred_element_type=jnp.float32
+        )
+        scores = jnp.sum(hidden * down_back, axis=1).astype(jnp.bfloat16).astype(jnp.float32)
+        column = lax.broadcasted_iota(jnp.int32, back.shape, 1)
+        partial_rows = jnp.where(column == width, scores[:, None], back).astype(jnp.bfloat16)
+        grads = (row_sum(feats, grad_both), row_sum(cotan, gated_hidden))
+        return partial_rows, grads
+
+    theirs, grads_theirs = rows_of(1 - core)
     swapped = lax.ppermute(theirs, "core", [(0, 1), (1, 0)])
+    mine, grads_mine = rows_of(core)
     pair = (mine.astype(jnp.float32) + swapped.astype(jnp.float32)).astype(jnp.bfloat16)
-    pair = pair.reshape(-1, partial_rows.shape[1])
     summed = lax.psum_scatter(pair, "chip", scatter_dimension=0, tiled=True)
-    both_grad = row_sum(feats, grad_both).astype(jnp.bfloat16)
+    both_grad = (grads_theirs[0] + grads_mine[0]).astype(jnp.bfloat16)
     gate_grad = both_grad[None, :, :hid]
     up_grad = both_grad[None, :, hid:]
-    down_grad = row_sum(cotan, gated_hidden).astype(jnp.bfloat16)[None]
+    down_grad = (grads_theirs[1] + grads_mine[1]).astype(jnp.bfloat16)[None]
     summed, gate_grad, up_grad, down_grad = lax.optimization_barrier(
         (summed, gate_grad, up_grad, down_grad)
     )

time: 245 us -> 245 us (level)
  matrix products: 30 us -> 42.1 us
  waiting for transfers between devices: 115 us -> 106 us
  other arithmetic: 17.1 us -> 14.2 us
    dot_general x3 -> x6, matrix products: 16 us -> 25.3 us  [the longest x2 11.6 us: rows_of(): down_back = jnp.dot(cotan, wdown, preferred_element_type=jnp.float32)]
    ppermute x1, waiting for transfers between devices: 6.25 us -> 0.01 us  [on_device(): swapped = lax.ppermute(theirs, 'core', [(0, 1), (1, 0)])]
    reduce_scatter x1, waiting for transfers between devices: 39.4 us -> 36.6 us  [on_device(): summed = lax.psum_scatter(pair, 'chip', scatter_dimension=0, tiled=True)]
    dot_general x2 -> x4, matrix products: 11.7 us -> 14.6 us  [row_sum(): lax.dot_general(left, right, (((0,), (0,)), ((), ())), preferred_element_...]
    convert_element_type x1 -> x0, other arithmetic: 2.62 us -> none  [on_device(): (mine.astype(jnp.float32) + swapped.astype(jnp.float32)).astype(jnp.bfloa...]
  transfers between devices with their start and end apart: 3 -> 3, of which waited for: 3 -> 2; matrix products, arithmetic and copies ran while one was open for 10% -> 15% of each run, Pallas kernels for 0% -> 0%
where the time goes in v7:
time: 245 us
  waiting for transfers between devices  106 us (43%)
  blocking collectives  59.5 us (24%)
  matrix products  42.1 us (17%)
  between operations  14.3 us (6%)
  other arithmetic  14.2 us (6%)
  local copies, waits for them, and re-layouts  8.17 us (3%)
    all_gather x1, waiting for transfers between devices, on_device(): gathered = lax.all_gather(recv, ('core', 'chip'), axis=0, tiled=True)  69.4 us
    reduce_scatter x1, waiting for transfers between devices, on_device(): summed = lax.psum_scatter(pair, 'chip', scatter_dimension=0, tiled=True)  36.6 us
    all_to_all x1, blocking collectives, on_device(): recv = lax.all_to_all(send, 'eg', split_axis=0, concat_axis=0, tiled=True)  36.3 us
    all_to_all x1, blocking collectives, on_device(): home = lax.all_to_all(summed, 'eg', split_axis=0, concat_axis=0, tiled=True)  23.2 us
    dot_general x4, matrix products, row_sum(): lax.dot_general(left, right, (((0,), (0,)), ((), ())), preferred_element_...  14.6 us
    dot_general x2, matrix products, rows_of(): down_back = jnp.dot(cotan, wdown, preferred_element_type=jnp.float32)  11.6 us
    convert_element_type x2, other arithmetic, dequantize(): return scaled.reshape(rows_in, cols_in).astype(jnp.bfloat16)  8.32 us
    dot_general x2, matrix products, rows_of(): both_pre = jnp.dot(feats, wboth, preferred_element_type=jnp.float32)  7.89 us
  transfers between devices with their start and end apart: 3, of which 2 were waited for; matrix products, arithmetic and copies ran while one was open for 15% of the time, Pallas kernels for 0%

profile of v7, /device:TPU:32, one launch (start us, length us, event | category | flops | bytes accessed | tf_op | source)
XLA Modules:
  0.0 244.9 jit_solution(4336218779786815597)
XLA Ops:
  7.2 0.0 all-gather.2.cloned.1.call-start
  7.2 0.8 fusion.43
  8.0 0.7 fusion.36
  8.7 0.7 bitcast_convert_fusion.4
  9.4 0.1 copy.52
  9.5 0.1 copy.29
  9.6 0.1 multiply_reduce_fusion.1
  9.8 0.1 copy.56
  9.8 0.1 copy.30
  10.0 1.4 convolution_convert_fusion
  11.4 0.1 fusion.27
  11.4 0.0 copy-start.3
  11.4 0.7 copy.31
  12.2 36.3 %all_to_all.10 = bf16[16,2,14464]{2,1,0:T(2,128)(2,1)S(1)} all-to-all(bf16[16,2,14464]{2,1,0:T(2,128)(2,1)S(1)} %copy.31), channel_id=1, replica_groups=mesh['eg'=16,'chip'=8,'core'=2] {'eg'}, dimensions={0} | all-to-all | bytes 1851392 | tf_op jit(solution)/shard_map/all_to_all | solution.py:79
  48.5 1.3 reshape.109
  49.7 0.0 all-gather.2.cloned.1.call-update
  49.8 0.0 reduce-scatter.2.cloned.1.call-start
  49.9 0.1 broadcast_bitcast_fusion.2
  49.9 0.1 broadcast_bitcast_fusion
  50.0 4.2 %fusion.8 = bf16[7168,128]{1,0:T(8,128)(2,1)S(1)} fusion(bf16[1,7168,128]{2,1,0:T(8,128)(2,1)} %param.13, f32[7168]{0:T(1024)S(1)} %get-tuple-element.27), kind=kLoop, calls=%fused_computation.18 | loop fusion | flops 2752512 | bytes 3698688 | tf_op jit(solution)/shard_map/convert_element_type | solution.py:17
  54.2 4.2 %fusion.9 = bf16[7168,128]{1,0:T(8,128)(2,1)S(1)} fusion(bf16[1,7168,128]{2,1,0:T(8,128)(2,1)} %param.12, f32[7168]{0:T(1024)S(1)} %broadcast_bitcast_fusion.2), kind=kLoop, calls=%fused_computation.20 | loop fusion | flops 2752512 | bytes 3698688 | tf_op jit(solution)/shard_map/convert_element_type | solution.py:17
  58.3 0.0 copy-start
  58.4 1.2 copy-done
  59.6 2.2 pad_maximum_fusion
  61.8 69.4 %all-gather.2.cloned.1.call-done = bf16[512,14464]{1,0:T(8,128)(2,1)} async-done(((bf16[32,14464]{1,0:T(8,128)(2,1)}), bf16[512,14464]{1,0:T(8,128)(2,1)}) %all-gather.2.cloned.1.call-update) | async-done | bytes 14811152 | tf_op jit(solution)/shard_map/all_gather | solution.py:87
  131.2 4.3 %fusion.14 = f32[256,256]{0,1:T(8,128)S(1)} fusion(bf16[512,14464]{1,0:T(8,128)(2,1)} %all-gather.2.cloned.1.call-done, s32[]{:T(128)S(6)} %select_n.15, bf16[7168,128]{1,0:T(8,128)(2,1)S(1)} %fusion.8, bf16[7168,128]{1,0:T(8,128)(2,1)} %copy-done), kind=kOutput, calls=%fused_computation.25 | convolution fusion | flops 946864128 | bytes 7602180 | tf_op jit(solution)/shard_map/dot_general | solution.py:96
  135.5 1.1 convert_reduce_fusion.1
  136.7 5.8 %multiply_convert_fusion.3 = (bf16[256,128]{0,1:T(8,128)(2,1)S(1)}, bf16[256,128]{0,1:T(8,128)(2,1)S(1)}, bf16[256]{0:T(256)(128)(2,1)S(1)}) fusion(f32[256,256]{0,1:T(8,128)S(1)} %fusion.14, f32[256]{0:T(256)S(1)} %get-tuple-element.14, bf16[1,7168,128]{2,1,0:T(8,128)(2,1)S(1)} %copy-done.4, f32[7168]{0:T(1024)S(1)} %get-tuple-element.26, ...), kind=kOutput, calls=%fused_computation.55 | convolution fusion | flops 473104128 | bytes 5928456 | tf_op jit(solution)/shard_map/dot_general | solution.py:97
  142.5 1.7 fusion.2
  144.2 0.5 collective-permute-start
  144.7 3.6 %fusion.17 = f32[256,256]{0,1:T(8,128)S(1)} fusion(bf16[512,14464]{1,0:T(8,128)(2,1)} %all-gather.2.cloned.1.call-done, s32[]{:T(128)S(6)} %select_n.13, bf16[7168,128]{1,0:T(8,128)(2,1)S(1)} %fusion.8, bf16[7168,128]{1,0:T(8,128)(2,1)S(1)} %copy-done.1), kind=kOutput, calls=%fused_computation.28 | convolution fusion | flops 946864128 | bytes 7602180 | tf_op jit(solution)/shard_map/dot_general | solution.py:96
  148.3 5.8 %multiply_convert_fusion.5 = (bf16[256,128]{0,1:T(8,128)(2,1)S(1)}, bf16[256,128]{0,1:T(8,128)(2,1)S(1)}, bf16[256]{0:T(256)(128)(2,1)S(1)}) fusion(f32[256,256]{0,1:T(8,128)S(1)} %fusion.17, f32[256]{0:T(256)S(1)} %get-tuple-element.13, bf16[1,7168,128]{2,1,0:T(8,128)(2,1)S(1)} %copy-done.4, f32[7168]{0:T(1024)S(1)} %get-tuple-element.26, ...), kind=kOutput, calls=%fused_computation.60 | convolution fusion | flops 473104128 | bytes 5928456 | tf_op jit(solution)/shard_map/dot_general | solution.py:97
  154.1 4.1 %add_convert_fusion = bf16[256,7296]{1,0:T(8,128)(2,1)} fusion(bf16[256,7296]{1,0:T(8,128)(2,1)S(1)} %collective-permute-done, bf16[256]{0:T(256)(128)(2,1)S(1)} %get-tuple-element.21, pred[7296]{0:T(1024)(128)(4,1)S(1)} %iota_compare_fusion.1, bf16[7168,256]{1,0:T(8,128)(2,1)S(1)} %copy-done.2, bf16[256,128]{0,1:T(8,128)(2,1)S(1)} %get-tuple-element.18, ...), kind=kOutput, calls=%fused_computation.13 | convolution fusion | flops 965902336 | bytes 11280000 | tf_op jit(solution)/shard_map/dot_general | solution.py:102
  158.2 0.0 reduce-scatter.2.cloned.1.call-update
  158.3 3.2 %fusion.12 = f32[7168,256]{1,0:T(8,128)S(1)} fusion(bf16[512,14464]{1,0:T(8,128)(2,1)} %all-gather.2.cloned.1.call-done, s32[]{:T(128)S(6)} %select_n.15, bf16[256,128]{0,1:T(8,128)(2,1)S(1)} %get-tuple-element.20, bf16[256,128]{0,1:T(8,128)(2,1)S(1)} %get-tuple-element.19), kind=kOutput, calls=%fused_computation.23 | convolution fusion | flops 939786240 | bytes 11141124 | tf_op jit(solution)/shard_map/dot_general | solution.py:57
  161.5 3.2 %fusion.19 = f32[7168,128]{1,0:T(8,128)S(1)} fusion(bf16[512,14464]{1,0:T(8,128)(2,1)} %all-gather.2.cloned.1.call-done, s32[]{:T(128)S(6)} %select_n.15, s32[]{:T(128)S(6)} %add.46, f32[256]{0:T(256)S(1)} %get-tuple-element.14, f32[256,256]{0,1:T(8,128)S(1)} %fusion.14), kind=kOutput, calls=%fused_computation.30 | convolution fusion | flops 469991424 | bytes 7603208 | tf_op jit(solution)/shard_map/dot_general | solution.py:57
  164.7 4.5 %fusion.5 = bf16[1,7168,128]{2,1,0:T(8,128)(2,1)} fusion(f32[7168,128]{1,0:T(8,128)S(1)} %fusion.19, bf16[512,14464]{1,0:T(8,128)(2,1)} %all-gather.2.cloned.1.call-done, s32[]{:T(128)S(6)} %select_n.13, s32[]{:T(128)S(6)} %add.46, f32[256]{0:T(256)S(1)} %get-tuple-element.13, f32[256,256]{0,1:T(8,128)S(1)} %fusion.17), kind=kOutput, calls=%fused_computation.10 | convolution fusion | flops 471826432 | bytes 9438216 | tf_op jit(solution)/shard_map/dot_general | solution.py:57
  169.2 3.6 %fusion.3 = bf16[7168,256]{1,0:T(8,128)(2,1)S(1)} fusion(f32[7168,256]{1,0:T(8,128)S(1)} %fusion.12, bf16[512,14464]{1,0:T(8,128)(2,1)} %all-gather.2.cloned.1.call-done, s32[]{:T(128)S(6)} %select_n.13, bf16[256,128]{0,1:T(8,128)(2,1)S(1)} %get-tuple-element.18, bf16[256,128]{0,1:T(8,128)(2,1)S(1)} %get-tuple-element.17), kind=kOutput, calls=%fused_computation.7 | convolution fusion | flops 943456256 | bytes 14811140 | tf_op jit(solution)/shard_map/dot_general | solution.py:57
  172.8 2.1 slice_bitcast_fusion
  174.9 36.6 %reduce-scatter.2.cloned.1.call-done = bf16[32,7296]{1,0:T(8,128)(2,1)} async-done(((bf16[256,7296]{1,0:T(8,128)(2,1)}), bf16[32,7296]{1,0:T(8,128)(2,1)}) %reduce-scatter.2.cloned.1.call-update) | async-done | bytes 466960 | tf_op jit(solution)/shard_map/reduce_scatter | solution.py:115
  211.5 1.2 reshape.110
  212.7 23.2 %all_to_all.11 = bf16[16,2,7296]{2,1,0:T(2,128)(2,1)S(1)} all-to-all(bf16[16,2,7296]{2,1,0:T(2,128)(2,1)S(1)} %reshape.110), channel_id=1, replica_groups=mesh['eg'=16,'chip'=8,'core'=2] {'eg'}, dimensions={0} | all-to-all | bytes 933888 | tf_op jit(solution)/shard_map/all_to_all | solution.py:124
  235.9 0.3 slice.74
  236.2 0.9 fusion.6
  237.1 0.1 copy.50
  237.2 0.1 copy.53
  237.3 0.2 multiply_reduce_fusion
  237.5 0.6 copy.49
  (16 shorter events, 0.1 us)
Async XLA Ops:
  7.2 124.0 %all-gather.2.cloned.1.call-start = ((), (), s32[]{:S(2)}) async-start(), calls=%async_computation.3 | async-start | bytes 15736832 | tf_op jit(solution)/shard_map/all_gather | solution.py:87
  11.4 38.4 %copy-start.3 = (bf16[1,3,1,56]{3,1,2,0:T(4,128)(2,1)S(1)}, bf16[1,3,1,56]{3,1,2,0:T(4,128)(2,1)}, u32[]{:S(2)}) copy-start(bf16[1,3,1,56]{3,1,2,0:T(4,128)(2,1)} %param.15) | copy-start | bytes 1012
  49.8 161.7 %reduce-scatter.2.cloned.1.call-start = ((), (), s32[]{:S(2)}) async-start(), calls=%async_computation.4 | async-start | bytes 4202496 | tf_op jit(solution)/shard_map/reduce_scatter | solution.py:115
  58.3 1.2 copy-start
  131.2 5.4 %copy-start.4 = (bf16[1,7168,128]{2,1,0:T(8,128)(2,1)S(1)}, bf16[1,7168,128]{2,1,0:T(8,128)(2,1)}, u32[]{:S(2)}) copy-start(bf16[1,7168,128]{2,1,0:T(8,128)(2,1)} %param.14) | copy-start | bytes 5505028
  135.5 7.0 %copy-start.2 = (bf16[7168,256]{1,0:T(8,128)(2,1)S(1)}, bf16[7168,256]{1,0:T(8,128)(2,1)}, u32[]{:S(2)}) copy-start(bf16[7168,256]{1,0:T(8,128)(2,1)} %pad_maximum_fusion) | copy-start | bytes 11010052
  142.5 2.2 copy-start.1
  144.2 9.9 %collective-permute-start = (bf16[256,7296]{1,0:T(8,128)(2,1)S(1)}, bf16[256,7296]{1,0:T(8,128)(2,1)S(1)}, u32[]{:S(2)}, u32[]{:S(2)}) collective-permute-start(bf16[256,7296]{1,0:T(8,128)(2,1)S(1)} %fusion.2), channel_id=1, source_target_pairs={{0,1},{1,0},{2,3},{3,2},{4,5},{5,4},{6,7},{7,6},{8,9},{9,8},{10,11... | collective-permute-start | bytes 11206664 | tf_op jit(solution)/shard_map/ppermute | solution.py:112
Sparse Core Ops, SparseCore 0:
  49.9 81.2 all-gather.1
  158.4 53.0 reduce-scatter.1
